TPU v7x, 256 devices: a whole 4x4x8 slice. The times are simulated.
256 devices in a mesh: req: 32 (over z, y_hi, core), tp: 8 (over x, y_lo).
Axes of the slice: x: 4, y: 4 (y_hi: 2, y_lo: 2; y = y_hi * 2 + y_lo), z: 8, core: 2. Of those that a mesh axis runs over, the one named last changes fastest.
Arguments:
- tokens: bfloat16 [16384, 1024], P(('req', 'tp')), may hold values from -6 to 6
- w_qkv: bfloat16 [1024, 3, 1024], P(None, None, 'tp'), may hold values from -0.1875 to 0.1875
- w_out: bfloat16 [1024, 1024], P('tp'), may hold values from -0.75 to 0.75
- w_up: bfloat16 [1024, 4096], P(None, 'tp'), may hold values from -0.1875 to 0.1875
- b_up: float32 [4096], P('tp'), may hold values from -4 to 4
- w_down: bfloat16 [4096, 1024], P('tp'), may hold values from -0.09375 to 0.09375
- b_down: float32 [1024], replicated, may hold values from -3 to 3
- ln1_gain: float32 [1024], replicated, may hold values from 0.5 to 1.5
- ln1_bias: float32 [1024], replicated, may hold values from -3 to 3
- ln2_gain: float32 [1024], replicated, may hold values from 0.5 to 1.5
- ln2_bias: float32 [1024], replicated, may hold values from -3 to 3
- kv_cache: bfloat16 [2, 32, 16384, 1024], P(None, None, 'req', 'tp'), may hold values from -122 to 122
- cache_len: int32 [32], replicated, may hold values from 0 to 16384, as said below
- span_len: int32 [32], replicated, may hold values from 1 to 512, as said below
Outputs:
- output: bfloat16 [16384, 1024], P(('req', 'tp'))
Inputs may be any that keep to these rules, and one draw needn't show every extreme that they name: The first cache_len[r] positions of request r hold its keys and values; some request has 16384. Slots from span_len[r] on are padding whose keys are not attended to; some request has 512.
All inputs are finite; a program needn't handle non-finite values.
Results may differ from a plain program's by a relative error of at most 0.015.
Values may be sent and summed in bfloat16 or wider, within the bound.
No kernel may reach another device: no remote copies, remote signals or barrier semaphores. Data moves between devices by JAX's collectives and lax.ppermute only.
A program may use at most 128 MiB of HBM per device.

v0:
```python
import jax
import jax.numpy as jnp
from jax import lax
from jax.sharding import PartitionSpec as P

HEAD_DIM = 64
SPAN = 512
REQ_DEV = 1


masked_score = -1e30


def layer_norm(values, gain, bias):
    centre = jnp.mean(values, axis=-1, keepdims=True)
    centred = values - centre
    variance = jnp.mean(centred * centred, axis=-1, keepdims=True)
    return centred * lax.rsqrt(variance + 1e-05) * gain + bias


def partial_attention(queries, key_rows, value_rows, allowed):
    scores = jnp.einsum(
        "chd,nhd->hcn", queries, key_rows, preferred_element_type=jnp.float32
    ) * queries.shape[-1] ** (-0.5)
    scores = jnp.where(allowed[None], scores, masked_score)
    peaks = jnp.max(scores, axis=-1)
    weights = jnp.where(allowed[None], jnp.exp(scores - peaks[..., None]), 0.0).astype(jnp.bfloat16)
    weight_sums = jnp.sum(weights.astype(jnp.float32), axis=-1)
    blended = jnp.einsum("hcn,nhd->chd", weights, value_rows, preferred_element_type=jnp.float32)
    return (peaks.T, weight_sums.T, blended.reshape(blended.shape[0], -1))


def merge_axis(peaks, weight_sums, blended, axis):
    highest = jnp.max(peaks, axis=axis, keepdims=True)
    factors = jnp.exp(peaks - highest)
    sums_out = jnp.sum(factors * weight_sums, axis=axis)
    spread = jnp.repeat(factors, blended.shape[-1] // peaks.shape[-1], axis=-1)
    blend_out = jnp.sum(spread * blended, axis=axis)
    return (jnp.squeeze(highest, axis=axis), sums_out, blend_out)


def block_partials(queries, key_rows, value_rows, starts, lengths):
    total_blocks = key_rows.shape[0]
    block_width = key_rows.shape[1]
    group_size = 2

    def single(one_query, one_keys, one_values, start_pos, limit):
        places = start_pos + jnp.arange(block_width, dtype=jnp.int32)
        allowed = jnp.broadcast_to((places < limit)[None, :], (one_query.shape[0], block_width))
        return partial_attention(one_query, one_keys, one_values, allowed)

    def grouped(items):
        return jax.vmap(single)(*items)

    def regroup(member):
        return member.reshape((total_blocks // group_size, group_size) + member.shape[1:])

    results = lax.map(
        grouped,
        (
            regroup(queries),
            regroup(key_rows),
            regroup(value_rows),
            regroup(starts),
            regroup(lengths),
        ),
    )
    return tuple((member.reshape((total_blocks,) + member.shape[2:]) for member in results))


def shards(
    tokens,
    w_qkv,
    w_out,
    w_up,
    b_up,
    w_down,
    b_down,
    ln1_gain,
    ln1_bias,
    ln2_gain,
    ln2_bias,
    kv_cache,
    cache_len,
    span_len,
):
    width_here = w_qkv.shape[2]
    heads_here = width_here // HEAD_DIM
    block_len = kv_cache.shape[2]
    flat_qkv = w_qkv.reshape(w_qkv.shape[0], 3 * width_here)
    heads_qkv = jnp.dot(
        lax.all_gather(tokens, "tp", axis=0, tiled=True),
        flat_qkv,
        preferred_element_type=jnp.float32,
    ).astype(jnp.bfloat16)
    local_shape = (REQ_DEV, SPAN, heads_here, HEAD_DIM)
    queries = heads_qkv[:, :width_here].reshape(local_shape)
    fresh_keys = heads_qkv[:, width_here : 2 * width_here].reshape(local_shape)
    fresh_values = heads_qkv[:, 2 * width_here :].reshape(local_shape)
    where_req = lax.axis_index("req")
    own_span_len = lax.dynamic_slice_in_dim(span_len, where_req * REQ_DEV, REQ_DEV)
    positions = jnp.arange(SPAN, dtype=jnp.int32)

    def own_partial(one_query, one_keys, one_values, limit):
        allowed = (positions[None, :] <= positions[:, None]) & (positions[None, :] < limit)
        return partial_attention(one_query, one_keys, one_values, allowed)

    fresh = jax.vmap(own_partial)(queries, fresh_keys, fresh_values, own_span_len)
    every_query = lax.all_gather(heads_qkv[:, :width_here], "req", axis=0, tiled=True)
    every_query = every_query.reshape(-1, SPAN, heads_here, HEAD_DIM)
    request_total = every_query.shape[0]
    cached = kv_cache.reshape(2, request_total, block_len, heads_here, HEAD_DIM)
    starts = jnp.full((request_total,), where_req * block_len, jnp.int32)
    peaks, weight_sums, blended = block_partials(
        every_query, cached[0], cached[1], starts, cache_len
    )
    got_blended = lax.all_to_all(blended[:, None], "req", split_axis=0, concat_axis=1, tiled=True)
    got_peaks = lax.all_to_all(peaks[:, None], "req", split_axis=0, concat_axis=1, tiled=True)
    got_sums = lax.all_to_all(weight_sums[:, None], "req", split_axis=0, concat_axis=1, tiled=True)
    peaks, weight_sums, blended = merge_axis(got_peaks, got_sums, got_blended, 1)
    peaks, weight_sums, blended = merge_axis(
        jnp.stack([fresh[0], peaks]),
        jnp.stack([fresh[1], weight_sums]),
        jnp.stack([fresh[2], blended]),
        0,
    )
    attention = (
        (blended / jnp.repeat(weight_sums, HEAD_DIM, axis=-1))
        .astype(jnp.bfloat16)
        .reshape(-1, width_here)
    )
    projected = lax.psum_scatter(
        jnp.dot(attention, w_out, preferred_element_type=jnp.float32).astype(jnp.bfloat16),
        "tp",
        scatter_dimension=0,
        tiled=True,
    ).astype(jnp.float32)
    normed = layer_norm(tokens.astype(jnp.float32) + projected, ln1_gain, ln1_bias).astype(
        jnp.bfloat16
    )
    hidden = jax.nn.gelu(
        jnp.dot(
            lax.all_gather(normed, "tp", axis=0, tiled=True),
            w_up,
            preferred_element_type=jnp.float32,
        )
        + b_up,
        approximate=False,
    ).astype(jnp.bfloat16)
    summed = lax.psum_scatter(
        jnp.dot(hidden, w_down, preferred_element_type=jnp.float32).astype(jnp.bfloat16),
        "tp",
        scatter_dimension=0,
        tiled=True,
    ).astype(jnp.float32)
    return layer_norm(summed + b_down + normed.astype(jnp.float32), ln2_gain, ln2_bias).astype(
        jnp.bfloat16
    )


def solution(mesh):
    placed = (
        P(("req", "tp"), None),
        P(None, None, "tp"),
        P("tp", None),
        P(None, "tp"),
        P("tp"),
        P("tp", None),
        P(),
        P(),
        P(),
        P(),
        P(),
        P(None, None, "req", "tp"),
        P(),
        P(),
    )
    return jax.shard_map(
        shards, mesh=mesh, in_specs=placed, out_specs=P(("req", "tp"), None), check_vma=False
    )
```

profile of v0, /device:TPU:80, one launch (start us, length us, event | category | flops | bytes accessed | tf_op | source)
XLA Modules:
  0.0 636.1 jit_solution(4704616808617209185)
XLA Ops:
  8.7 44.3 %all-gather.4.cloned.1.call-done = bf16[512,1024]{1,0:T(8,128)(2,1)} async-done(((bf16[64,1024]{1,0:T(8,128)(2,1)}), bf16[512,1024]{1,0:T(8,128)(2,1)}) %all-gather.4.cloned.1.call-update) | async-done | bytes 1048592 | tf_op jit(solution)/shard_map/all_gather | solution.py:92
  55.7 6.0 fusion.95
  61.7 6.5 %copy.29 = bf16[1,32,512,128]{2,3,1,0:T(8,128)(2,1)} copy(bf16[1,32,512,128]{3,2,1,0:T(8,128)(2,1)} %get-tuple-element.106) | data formatting | bytes 8388608 | tf_op jit(solution)/shard_map/slice | solution.py:115
  68.2 6.5 %copy.28 = bf16[1,32,512,128]{2,3,1,0:T(8,128)(2,1)} copy(bf16[1,32,512,128]{3,2,1,0:T(8,128)(2,1)} %get-tuple-element.107) | data formatting | bytes 8388608 | tf_op jit(solution)/shard_map/slice | solution.py:115
  74.7 63.5 %all-gather.6.cloned.1.call-done = bf16[16384,128]{0,1:T(8,128)(2,1)} async-done(((bf16[512,128]{0,1:T(8,128)(2,1)}), bf16[16384,128]{0,1:T(8,128)(2,1)}) %all-gather.6.cloned.1.call-update) | async-done | bytes 4194320 | tf_op jit(solution)/shard_map/all_gather | solution.py:109
  138.2 7.8 %reshape_reshape.3 = bf16[16,2,512,2,64]{2,1,0,4,3:T(2,128)(2,1)} reshape(bf16[16384,128]{0,1:T(8,128)(2,1)} %all-gather.6.cloned.1.call-done) | data formatting | bytes 8388608 | tf_op jit(solution)/shard_map/reshape;reshape | solution.py:56
  146.0 115.6 %while.14 = (s32[]{:T(128)}, f32[16,2,512,2]{2,3,1,0:T(2,128)S(1)}, f32[16,2,512,2]{2,3,1,0:T(2,128)S(1)}, f32[16,2,512,128]{2,3,1,0:T(8,128)}, s32[16,2]{1,0:T(...) while((s32[]{:T(128)}, f32[16,2,512,2]{2,3,1,0:T(2,128)S(1)}, ...), condition=%wide.region_4.5_spmd, body=%wide.region_1.4_spmd.sunk | while | flops 284162048 | bytes 15536313 | solution.py:58
  150.2 2.1 fusion.116
  157.4 2.1 fusion.116
  164.7 2.1 fusion.116
  171.9 2.1 fusion.116
  179.2 2.1 fusion.116
  186.4 2.1 fusion.116
  193.6 2.1 fusion.116
  200.8 2.1 fusion.116
  208.1 2.1 fusion.116
  215.3 2.1 fusion.116
  222.5 2.1 fusion.116
  229.7 2.1 fusion.116
  237.0 2.1 fusion.116
  244.2 2.1 fusion.116
  251.4 2.1 fusion.116
  258.6 2.1 fusion.116
  261.6 15.7 %all_to_all.36 = f32[32,1,512,2]{2,3,1,0:T(2,128)S(1)} all-to-all(f32[32,1,512,2]{2,3,1,0:T(2,128)S(1)} %bitcast.115), channel_id=1, replica_groups=mesh['req'=32,'tp'=8] {'req'}, dimensions={0} | all-to-all | bytes 262144 | tf_op jit(solution)/shard_map/all_to_all | solution.py:118
  277.3 14.1 %all_to_all.37 = f32[32,1,512,2]{2,3,1,0:T(2,128)S(1)} all-to-all(f32[32,1,512,2]{2,3,1,0:T(2,128)S(1)} %bitcast.114), channel_id=1, replica_groups=mesh['req'=32,'tp'=8] {'req'}, dimensions={0} | all-to-all | bytes 262144 | tf_op jit(solution)/shard_map/all_to_all | solution.py:119
  291.3 8.5 %all-to-all-start.1 = ((f32[32,1,512,128]{2,3,1,0:T(8,128)}), f32[32,1,512,128]{2,3,1,0:T(8,128)}, u32[]{:S(2)}, u32[]{:S(2)}) async-start(f32[32,1,512,128]{2,3,1,0:T(8,128)} %bitcast.105), calls=%async_computation.1 | async-start | bytes 16777216 | tf_op jit(solution)/shard_map/all_to_all | solution.py:117
  303.7 181.2 %all-to-all-done.1 = f32[32,1,512,128]{2,3,1,0:T(8,128)} async-done(((f32[32,1,512,128]{2,3,1,0:T(8,128)}), f32[32,1,512,128]{2,3,1,0:T(8,128)}, u32[]{:S(2)}, u32[]{:S(2)}) %all-to-all-start.1) | async-done | bytes 8388640 | tf_op jit(solution)/shard_map/all_to_all | solution.py:117
  486.0 5.4 multiply_reduce_fusion
  493.0 40.7 %reduce-scatter.3.cloned.1.call-done = bf16[64,1024]{1,0:T(8,128)(2,1)} async-done(((bf16[512,1024]{1,0:T(8,128)(2,1)}), bf16[64,1024]{1,0:T(8,128)(2,1)}) %reduce-scatter.3.cloned.1.call-update) | async-done | bytes 131088 | tf_op jit(solution)/shard_map/reduce_scatter | solution.py:132
  537.7 41.0 %all-gather.8.cloned.1.call-done = bf16[512,1024]{1,0:T(8,128)(2,1)} async-done(((bf16[64,1024]{1,0:T(8,128)(2,1)}), bf16[512,1024]{1,0:T(8,128)(2,1)}) %all-gather.8.cloned.1.call-update) | async-done | bytes 1048592 | tf_op jit(solution)/shard_map/all_gather | solution.py:143
  578.7 5.6 convolution_convert_fusion.1
  584.4 41.3 %reduce-scatter.5.cloned.1.call-done = bf16[64,1024]{1,0:T(8,128)(2,1)} async-done(((bf16[512,1024]{1,0:T(8,128)(2,1)}), bf16[64,1024]{1,0:T(8,128)(2,1)}) %reduce-scatter.5.cloned.1.call-update) | async-done | bytes 131088 | tf_op jit(solution)/shard_map/reduce_scatter | solution.py:150
  (200 shorter events, 100.5 us)
Async XLA Ops:
  6.5 572.2 %copy-start = (bf16[512,1024]{1,0:T(8,128)(2,1)S(1)}, bf16[512,1024]{1,0:T(8,128)(2,1)}, u32[]{:S(2)}) copy-start(bf16[512,1024]{1,0:T(8,128)(2,1)} %param.21) | copy-start | bytes 3145732
  6.5 49.1 %copy-start.10 = (s32[32]{0:T(128)S(1)}, s32[32]{0:T(128)}, u32[]{:S(2)}) copy-start(s32[32]{0:T(128)} %param.28) | copy-start | bytes 388
  6.5 46.5 %all-gather.4.cloned.1.call-start = ((), (), s32[]{:S(2)}) async-start(), calls=%async_computation.5 | async-start | bytes 1179648 | tf_op jit(solution)/shard_map/all_gather | solution.py:92
  7.3 130.9 %all-gather.6.cloned.1.call-start = ((), (), s32[]{:S(2)}) async-start(), calls=%async_computation.6 | async-start | bytes 4325376 | tf_op jit(solution)/shard_map/all_gather | solution.py:109
  291.3 8.8 %copy-start.13 = (s32[32]{0:T(128)S(1)}, s32[32]{0:T(128)}, u32[]{:S(2)}) copy-start(s32[32]{0:T(128)} %param.29) | copy-start | bytes 388
  291.3 10.1 %copy-start.3 = (bf16[512,128]{0,1:T(8,128)(2,1)S(1)}, bf16[512,128]{0,1:T(8,128)(2,1)}, u32[]{:S(2)}) copy-start(bf16[512,128]{0,1:T(8,128)(2,1)} %get-tuple-element.110) | copy-start | bytes 393220
  291.3 193.5 %all-to-all-start.1 = ((f32[32,1,512,128]{2,3,1,0:T(8,128)}), f32[32,1,512,128]{2,3,1,0:T(8,128)}, u32[]{:S(2)}, u32[]{:S(2)}) async-start(f32[32,1,512,128]{2,3,1,0:T(8,128)} %bitcast.105), calls=%async_computation.1 | async-start | bytes 16777216 | tf_op jit(solution)/shard_map/all_to_all | solution.py:117
  299.9 233.9 %reduce-scatter.3.cloned.1.call-start = ((), (), s32[]{:S(2)}) async-start(), calls=%async_computation.7 | async-start | bytes 1179648 | tf_op jit(solution)/shard_map/reduce_scatter | solution.py:132
  485.9 5.6 copy-start.4
  485.9 47.8 %copy-start.2 = (bf16[64,1024]{1,0:T(8,128)(2,1)S(1)}, bf16[64,1024]{1,0:T(8,128)(2,1)}, u32[]{:S(2)}) copy-start(bf16[64,1024]{1,0:T(8,128)(2,1)} %param.16) | copy-start | bytes 393220
  491.4 44.6 %copy-start.6 = (f32[1024]{0:T(1024)S(1)}, f32[1024]{0:T(1024)}, u32[]{:S(2)}) copy-start(f32[1024]{0:T(1024)} %param.24) | copy-start | bytes 12292
  491.4 44.6 %copy-start.7 = (f32[1024]{0:T(1024)S(1)}, f32[1024]{0:T(1024)}, u32[]{:S(2)}) copy-start(f32[1024]{0:T(1024)} %param.23) | copy-start | bytes 12292
  491.4 87.3 %copy-start.11 = (bf16[1024,512]{1,0:T(8,128)(2,1)S(1)}, bf16[1024,512]{1,0:T(8,128)(2,1)}, u32[]{:S(2)}) copy-start(bf16[1024,512]{1,0:T(8,128)(2,1)} %param.19) | copy-start | bytes 3145732
  491.4 87.3 %copy-start.12 = (f32[512]{0:T(512)S(1)}, f32[512]{0:T(512)}, u32[]{:S(2)}) copy-start(f32[512]{0:T(512)} %param.20) | copy-start | bytes 6148
  493.0 85.7 %all-gather.8.cloned.1.call-start = ((), (), s32[]{:S(2)}) async-start(), calls=%async_computation.8 | async-start | bytes 1179648 | tf_op jit(solution)/shard_map/all_gather | solution.py:143
  537.6 88.0 %copy-start.1 = (bf16[64,1024]{1,0:T(8,128)(2,1)S(1)}, bf16[64,1024]{1,0:T(8,128)(2,1)}, u32[]{:S(2)}) copy-start(bf16[64,1024]{1,0:T(8,128)(2,1)} %add_convert_fusion.1) | copy-start | bytes 393220
  537.7 88.0 %copy-start.5 = (f32[1024]{0:T(1024)S(1)}, f32[1024]{0:T(1024)}, u32[]{:S(2)}) copy-start(f32[1024]{0:T(1024)} %param.22) | copy-start | bytes 12292
  537.7 90.2 %copy-start.8 = (f32[1024]{0:T(1024)S(1)}, f32[1024]{0:T(1024)}, u32[]{:S(2)}) copy-start(f32[1024]{0:T(1024)} %param.26) | copy-start | bytes 12292
  537.7 90.2 %copy-start.9 = (f32[1024]{0:T(1024)S(1)}, f32[1024]{0:T(1024)}, u32[]{:S(2)}) copy-start(f32[1024]{0:T(1024)} %param.25) | copy-start | bytes 12292
  537.7 88.0 %reduce-scatter.5.cloned.1.call-start = ((), (), s32[]{:S(2)}) async-start(), calls=%async_computation.9 | async-start | bytes 1179648 | tf_op jit(solution)/shard_map/reduce_scatter | solution.py:150
Sparse Core Ops, SparseCore 0:
  9.2 43.8 all-gather.3
  55.7 82.4 all-gather.5
  493.1 40.5 reduce-scatter.2
  537.8 40.9 all-gather.7
  584.5 41.1 reduce-scatter.4
where the time goes:
time: 639 us; the launch traced here: 636 us
  waiting for transfers between devices  413 us (65%)
  matrix products  75.5 us (12%)
  local copies, waits for them, and re-layouts  62.7 us (10%)
  other arithmetic  32.9 us (5%)
  blocking collectives  29.7 us (5%)
  between operations  13.5 us (2%)
  starting transfers between devices  8.86 us (1%)
    all_to_all x1, waiting for transfers between devices, shards(): lax.all_to_all(blended[:, None], 'req', split_axis=0, concat_axis=1, tile...  181 us
    all_gather x1, waiting for transfers between devices, shards(): lax.all_gather(heads_qkv[:, :width_here], 'req', axis=0, tiled=True)  63.5 us
    all_gather x1, waiting for transfers between devices, shards(): lax.all_gather(tokens, 'tp', axis=0, tiled=True)  44.3 us
    reduce_scatter x1, waiting for transfers between devices, shards(): lax.psum_scatter(jnp.dot(hidden, w_down, preferred_element_type=jnp.float...  41.3 us
    all_gather x1, waiting for transfers between devices, shards(): lax.all_gather(normed, 'tp', axis=0, tiled=True)  41 us
    reduce_scatter x1, waiting for transfers between devices, shards(): lax.psum_scatter(jnp.dot(attention, w_out, preferred_element_type=jnp.flo...  40.7 us
    dot_general x17, matrix products, partial_attention(): jnp.einsum('hcn,nhd->chd', weights, value_rows, preferred_element_type=jn...  34.6 us
    dot_general x17, matrix products, partial_attention(): jnp.einsum('chd,nhd->hcn', queries, key_rows, preferred_element_type=jnp....  32 us
  transfers between devices with their start and end apart: 6, of which 6 were waited for; matrix products, arithmetic and copies ran while one was open for 4% of the time, Pallas kernels for 0%

commit v1 on v0

v1 whole, which is shorter than its diff:
```python
import jax
import jax.numpy as jnp
from jax import lax
from jax.sharding import PartitionSpec as P

HEAD_DIM = 64
BLOCK_GROUP = 4

masked_score = -1e30


def layer_norm(values, gain, bias):
    centre = jnp.mean(values, axis=-1, keepdims=True)
    centred = values - centre
    variance = jnp.mean(centred * centred, axis=-1, keepdims=True)
    return centred * lax.rsqrt(variance + 1e-05) * gain + bias


def partial_attention(queries, key_rows, value_rows, allowed):
    scores = jnp.einsum(
        "chd,nhd->hcn", queries, key_rows, preferred_element_type=jnp.float32
    ) * queries.shape[-1] ** (-0.5)
    scores = jnp.where(allowed[None], scores, masked_score)
    peaks = jnp.max(scores, axis=-1)
    weights = jnp.where(allowed[None], jnp.exp(scores - peaks[..., None]), 0.0).astype(jnp.bfloat16)
    weight_sums = jnp.sum(weights.astype(jnp.float32), axis=-1)
    blended = jnp.einsum("hcn,nhd->chd", weights, value_rows, preferred_element_type=jnp.float32)
    return (peaks.T, weight_sums.T, blended.reshape(blended.shape[0], -1))


def merge_axis(peaks, weight_sums, blended, axis):
    highest = jnp.max(peaks, axis=axis, keepdims=True)
    factors = jnp.exp(peaks - highest)
    sums_out = jnp.sum(factors * weight_sums, axis=axis)
    spread = jnp.repeat(factors, blended.shape[-1] // peaks.shape[-1], axis=-1)
    blend_out = jnp.sum(spread * blended, axis=axis)
    return (jnp.squeeze(highest, axis=axis), sums_out, blend_out)


def cache_partials(queries, keys, values, cached_count):
    total_blocks, block_width = keys.shape[0], keys.shape[1]
    group = BLOCK_GROUP if total_blocks % BLOCK_GROUP == 0 else 1

    def single(one_keys, one_values, block):
        places = block * block_width + jnp.arange(block_width, dtype=jnp.int32)
        allowed = jnp.broadcast_to((places < cached_count)[None, :], (queries.shape[0], block_width))
        return partial_attention(queries, one_keys, one_values, allowed)

    def grouped(items):
        return jax.vmap(single)(*items)

    def regroup(member):
        return member.reshape((total_blocks // group, group) + member.shape[1:])

    results = lax.map(
        grouped,
        (regroup(keys), regroup(values), regroup(jnp.arange(total_blocks, dtype=jnp.int32))),
    )
    return tuple(member.reshape((total_blocks,) + member.shape[2:]) for member in results)


def shards(
    tokens,
    w_qkv,
    w_out,
    w_up,
    b_up,
    w_down,
    b_down,
    ln1_gain,
    ln1_bias,
    ln2_gain,
    ln2_bias,
    kv_cache,
    cache_len,
    span_len,
):
    width_here = w_qkv.shape[2]
    heads_here = width_here // HEAD_DIM
    where_req = lax.axis_index("req")

    own_cache = lax.all_to_all(kv_cache, "req", split_axis=1, concat_axis=1, tiled=True)

    span_rows = lax.all_gather(tokens, "tp", axis=0, tiled=True)
    flat_qkv = w_qkv.reshape(w_qkv.shape[0], 3 * width_here)
    heads_qkv = jnp.dot(span_rows, flat_qkv, preferred_element_type=jnp.float32).astype(jnp.bfloat16)
    span = heads_qkv.shape[0]
    local_shape = (span, heads_here, HEAD_DIM)
    queries = heads_qkv[:, :width_here].reshape(local_shape)
    fresh_keys = heads_qkv[:, width_here : 2 * width_here].reshape(local_shape)
    fresh_values = heads_qkv[:, 2 * width_here :].reshape(local_shape)

    full_out = lax.all_gather(w_out, "tp", axis=0, tiled=True)
    full_up = lax.all_gather(w_up, "tp", axis=1, tiled=True)
    full_b_up = lax.all_gather(b_up, "tp", axis=0, tiled=True)
    full_down = lax.all_gather(w_down, "tp", axis=0, tiled=True)

    fresh_count = span_len[where_req]
    cached_count = cache_len[where_req]
    positions = jnp.arange(span, dtype=jnp.int32)
    allowed = (positions[None, :] <= positions[:, None]) & (positions[None, :] < fresh_count)
    fresh = partial_attention(queries, fresh_keys, fresh_values, allowed)

    total_blocks, block_width = own_cache.shape[1], own_cache.shape[2]
    cached = own_cache.reshape(2, total_blocks, block_width, heads_here, HEAD_DIM)
    peaks, weight_sums, blended = cache_partials(queries, cached[0], cached[1], cached_count)
    peaks, weight_sums, blended = merge_axis(
        jnp.concatenate([fresh[0][None], peaks]),
        jnp.concatenate([fresh[1][None], weight_sums]),
        jnp.concatenate([fresh[2][None], blended]),
        0,
    )
    attention = (blended / jnp.repeat(weight_sums, HEAD_DIM, axis=-1)).astype(jnp.bfloat16)
    attention = lax.all_to_all(attention, "tp", split_axis=0, concat_axis=1, tiled=True)

    projected = jnp.dot(attention, full_out, preferred_element_type=jnp.float32)
    normed = layer_norm(tokens.astype(jnp.float32) + projected, ln1_gain, ln1_bias).astype(jnp.bfloat16)
    hidden = jax.nn.gelu(
        jnp.dot(normed, full_up, preferred_element_type=jnp.float32) + full_b_up,
        approximate=False,
    ).astype(jnp.bfloat16)
    summed = jnp.dot(hidden, full_down, preferred_element_type=jnp.float32) + b_down + normed.astype(jnp.float32)
    return layer_norm(summed, ln2_gain, ln2_bias).astype(jnp.bfloat16)


def solution(mesh):
    placed = (
        P(("req", "tp"), None),
        P(None, None, "tp"),
        P("tp", None),
        P(None, "tp"),
        P("tp"),
        P("tp", None),
        P(),
        P(),
        P(),
        P(),
        P(),
        P(None, None, "req", "tp"),
        P(),
        P(),
    )
    return jax.shard_map(
        shards, mesh=mesh, in_specs=placed, out_specs=P(("req", "tp"), None), check_vma=False
    )
```

time: 639 us -> 561 us (0.88)
  local copies, waits for them, and re-layouts: 62.7 us -> 29.5 us
  waiting for transfers between devices: 413 us -> 380 us
  matrix products: 75.5 us -> 55.5 us
  starting transfers between devices: 8.86 us -> 15.4 us
    reduce_scatter x2 -> x0, waiting for transfers between devices: 82 us -> none  [the longest x1 41.3 us: shards(): lax.psum_scatter(jnp.dot(hidden, w_down, preferred_element_type=jnp.float...]
    all_gather x3 -> x4, waiting for transfers between devices: 149 us -> 227 us  [the longest x1 177 us: shards(): full_up = lax.all_gather(w_up, 'tp', axis=1, tiled=True)]
    all_to_all x1 -> x2, waiting for transfers between devices: 181 us -> 150 us  [the longest x1 150 us: shards(): lax.all_to_all(kv_cache, 'req', split_axis=1, concat_axis=1, tiled=True)]
    all_to_all x2 -> x0, blocking collectives: 29.7 us -> none  [the longest x1 15.7 us: shards(): lax.all_to_all(peaks[:, None], 'req', split_axis=0, concat_axis=1, tiled=...]
    all_gather x0 -> x1, blocking collectives: none -> 26.2 us  [shards(): full_b_up = lax.all_gather(b_up, 'tp', axis=0, tiled=True)]
    dot_general x17 -> x9, matrix products: 34.6 us -> 15.8 us  [partial_attention(): jnp.einsum('hcn,nhd->chd', weights, value_rows, preferred_element_type=jn...]
    dynamic_slice x17 -> x2, local copies, waits for them, and re-layouts: 18.7 us -> 1.33 us  [the longest x1 0.67 us: shards(): cached_count = cache_len[where_req]]
    unnamed x29 -> x22, local copies, waits for them, and re-layouts: 1.48 us -> 12.3 us
  transfers between devices with their start and end apart: 6 -> 6, of which waited for: 6 -> 4; matrix products, arithmetic and copies ran while one was open for 4% -> 19% of each run, Pallas kernels for 0% -> 0%
where the time goes in v1:
time: 561 us; the launch traced here: 554 us
  waiting for transfers between devices  380 us (68%)
  matrix products  55.5 us (10%)
  other arithmetic  33.7 us (6%)
  local copies, waits for them, and re-layouts  29.5 us (5%)
  blocking collectives  26.2 us (5%)
  starting transfers between devices  15.4 us (3%)
  between operations  13.4 us (2%)
    all_gather x1, waiting for transfers between devices, shards(): full_up = lax.all_gather(w_up, 'tp', axis=1, tiled=True)  177 us
    all_to_all x1, waiting for transfers between devices, shards(): lax.all_to_all(kv_cache, 'req', split_axis=1, concat_axis=1, tiled=True)  150 us
    all_gather x1, waiting for transfers between devices, shards(): span_rows = lax.all_gather(tokens, 'tp', axis=0, tiled=True)  28.4 us
    all_gather x1, blocking collectives, shards(): full_b_up = lax.all_gather(b_up, 'tp', axis=0, tiled=True)  26.2 us
    dot_general x9, matrix products, partial_attention(): jnp.einsum('chd,nhd->hcn', queries, key_rows, preferred_element_type=jnp....  24.5 us
    all_gather x1, waiting for transfers between devices, shards(): full_down = lax.all_gather(w_down, 'tp', axis=0, tiled=True)  21.2 us
    reduce_sum x9, other arithmetic, partial_attention(): weight_sums = jnp.sum(weights.astype(jnp.float32), axis=-1)  21.2 us
    dot_general x9, matrix products, partial_attention(): jnp.einsum('hcn,nhd->chd', weights, value_rows, preferred_element_type=jn...  15.8 us
  transfers between devices with their start and end apart: 6, of which 4 were waited for; matrix products, arithmetic and copies ran while one was open for 19% of the time, Pallas kernels for 0%

profile of v1, /device:TPU:80, one launch (start us, length us, event | category | flops | bytes accessed | tf_op | source)
XLA Modules:
  0.0 553.8 jit_solution(13664042874538674882)
XLA Ops:
  8.7 12.0 %copy.29 = bf16[2,32,512,128]{2,3,0,1:T(8,128)(2,1)} copy(bf16[2,32,512,128]{3,2,1,0:T(8,128)(2,1)} %param.27) | data formatting | bytes 16777216 | tf_op args[11]
  20.7 10.9 %all-to-all-start = ((bf16[2,32,512,128]{2,3,0,1:T(8,128)(2,1)}), bf16[2,32,512,128]{2,3,0,1:T(8,128)(2,1)}, u32[]{:S(2)}, u32[]{:S(2)}) async-start(bf16[2,32,512,128]{2,3,0,1:T(8,128)(2,1)} %copy.29), calls=%async_computation | async-start | bytes 16777216 | tf_op jit(solution)/shard_map/all_to_all | solution.py:82
  34.7 28.4 %all-gather.6.cloned.1.call-done = bf16[512,1024]{1,0:T(8,128)(2,1)} async-done(((bf16[64,1024]{1,0:T(8,128)(2,1)}), bf16[512,1024]{1,0:T(8,128)(2,1)}) %all-gather.6.cloned.1.call-update) | async-done | bytes 1048592 | tf_op jit(solution)/shard_map/all_gather | solution.py:84
  67.0 150.2 %all-to-all-done = bf16[2,32,512,128]{2,3,0,1:T(8,128)(2,1)} async-done(((bf16[2,32,512,128]{2,3,0,1:T(8,128)(2,1)}), bf16[2,32,512,128]{2,3,0,1:T(8,128)(2,1)}, u32[]{:S(2)}, u32[]{:S(2)}) %all-to-all-start) | async-done | bytes 8388640 | tf_op jit(solution)/shard_map/all_to_all | solution.py:82
  217.1 5.9 %fusion.101 = (bf16[1,32,512,128]{2,3,0,1:T(8,128)(2,1)}, bf16[1,32,512,128]{2,3,0,1:T(8,128)(2,1)}) fusion(bf16[2,32,512,128]{2,3,0,1:T(8,128)(2,1)} %all-to-all-done), kind=kLoop, calls=%fused_computation.139 | loop fusion | bytes 16777216 | tf_op jit(solution)/shard_map/slice | solution.py:106
  223.1 74.7 %while.14 = (s32[]{:T(128)}, f32[8,4,512,2]{2,1,3,0:T(4,128)S(1)}, f32[8,4,512,2]{2,3,1,0:T(2,128)S(1)}, f32[8,4,512,128]{2,3,1,0:T(8,128)}, s32[8,4]{1,0:T(8,12...) while((s32[]{:T(128)}, f32[8,4,512,2]{2,1,3,0:T(4,128)S(1)}, ...), condition=%wide.region_4.5_spmd, body=%wide.region_1.4_spmd.sunk | while | flops 557838336 | bytes 29612216 | solution.py:55
  223.8 3.0 bitcast_reduce_fusion.2
  226.8 2.6 convert_reduce_fusion.3
  229.4 1.9 fusion.121
  233.2 3.0 bitcast_reduce_fusion.2
  236.2 2.6 convert_reduce_fusion.3
  238.8 1.9 fusion.121
  242.5 3.0 bitcast_reduce_fusion.2
  245.5 2.6 convert_reduce_fusion.3
  251.8 3.0 bitcast_reduce_fusion.2
  254.9 2.6 convert_reduce_fusion.3
  261.2 3.0 bitcast_reduce_fusion.2
  264.2 2.6 convert_reduce_fusion.3
  270.5 3.0 bitcast_reduce_fusion.2
  273.5 2.6 convert_reduce_fusion.3
  276.2 1.9 fusion.121
  279.9 3.0 bitcast_reduce_fusion.2
  282.9 2.6 convert_reduce_fusion.3
  289.2 3.0 bitcast_reduce_fusion.2
  292.2 2.6 convert_reduce_fusion.3
  298.1 4.2 fusion.12
  303.3 4.4 all-to-all-start.1
  307.8 26.2 %all-gather = f32[8,1,512]{2,1,0:T(1,128)S(1)} all-gather(f32[1,1,512]{2,1,0:T(1,128)S(1)} %bitcast.114), channel_id=1, replica_groups=mesh['req'=32,'tp'=8] {'tp'}, dimensions={0}, use_global_device_ids=true | all-gather | bytes 18432 | tf_op jit(solution)/shard_map/all_gather | solution.py:95
  334.1 2.2 fusion.103
  336.5 21.2 %all-gather.12.cloned.1.call-done = bf16[4096,1024]{1,0:T(8,128)(2,1)} async-done(((bf16[512,1024]{1,0:T(8,128)(2,1)}), bf16[4096,1024]{1,0:T(8,128)(2,1)}) %all-gather.12.cloned.1.call-update) | async-done | bytes 8388624 | tf_op jit(solution)/shard_map/all_gather | solution.py:96
  357.7 177.4 %all-gather.10.cloned.1.call-done = bf16[1024,4096]{1,0:T(8,128)(2,1)} async-done(((bf16[1024,512]{1,0:T(8,128)(2,1)}), bf16[1024,4096]{1,0:T(8,128)(2,1)}) %all-gather.10.cloned.1.call-update) | async-done | bytes 8388624 | tf_op jit(solution)/shard_map/all_gather | solution.py:94
  535.1 11.1 %fusion.104 = (f32[64]{0:T(128)S(1)}, f32[64,1024]{1,0:T(8,128)S(1)}) fusion(f32[1024]{0:T(1024)S(1)} %copy-done.5, f32[1024]{0:T(1024)S(1)} %copy-done.6, f32[64]{0:T(128)S(1)} %add_rsqrt_fusion.1, f32[64,1024]{1,0:T(8,128)S(1)} %get-tuple-element.116, f32[64]{0:T(128)S(1)} %broadcast_multiply_fusion.1, f32[1024]{0:T(1024)S(1)} %copy-done.7, ...), kind=kOutput, calls=%fused_computation.142 | convolution fusion | flops 1091960832 | bytes 17330944 | tf_op jit(solution)/shard_map/dot_general | solution.py:122
  (103 shorter events, 35.9 us)
Async XLA Ops:
  6.5 56.6 %all-gather.6.cloned.1.call-start = ((), (), s32[]{:S(2)}) async-start(), calls=%async_computation.2 | async-start | bytes 1179648 | tf_op jit(solution)/shard_map/all_gather | solution.py:84
  7.3 326.8 %all-gather.8.cloned.1.call-start = ((), (), s32[]{:S(2)}) async-start(), calls=%async_computation.3 | async-start | bytes 2359296 | tf_op jit(solution)/shard_map/all_gather | solution.py:93
  8.0 349.7 %all-gather.12.cloned.1.call-start = ((), (), s32[]{:S(2)}) async-start(), calls=%async_computation.5 | async-start | bytes 9437184 | tf_op jit(solution)/shard_map/all_gather | solution.py:96
  20.7 11.5 %copy-start = (bf16[1024,3,128]{2,0,1:T(8,128)(2,1)S(1)}, bf16[1024,3,128]{2,0,1:T(8,128)(2,1)}, u32[]{:S(2)}) copy-start(bf16[1024,3,128]{2,0,1:T(8,128)(2,1)} %param.17) | copy-start | bytes 2359300
  20.7 11.8 %copy-start.8 = (s32[32]{0:T(128)S(1)}, s32[32]{0:T(128)}, u32[]{:S(2)}) copy-start(s32[32]{0:T(128)} %param.28) | copy-start | bytes 388
  20.7 12.5 %copy-start.9 = (s32[32]{0:T(128)S(1)}, s32[32]{0:T(128)}, u32[]{:S(2)}) copy-start(s32[32]{0:T(128)} %param.29) | copy-start | bytes 388
  20.7 196.4 %all-to-all-start = ((bf16[2,32,512,128]{2,3,0,1:T(8,128)(2,1)}), bf16[2,32,512,128]{2,3,0,1:T(8,128)(2,1)}, u32[]{:S(2)}, u32[]{:S(2)}) async-start(bf16[2,32,512,128]{2,3,0,1:T(8,128)(2,1)} %copy.29), calls=%async_computation | async-start | bytes 16777216 | tf_op jit(solution)/shard_map/all_to_all | solution.py:82
  31.6 503.5 %all-gather.10.cloned.1.call-start = ((), (), s32[]{:S(2)}) async-start(), calls=%async_computation.4 | async-start | bytes 9437184 | tf_op jit(solution)/shard_map/all_gather | solution.py:94
  298.1 9.7 %copy-start.4 = (f32[512]{0:T(512)S(1)}, f32[512]{0:T(512)}, u32[]{:S(2)}) copy-start(f32[512]{0:T(512)} %param.20) | copy-start | bytes 6148
  298.1 36.0 %copy-start.1 = (bf16[64,1024]{1,0:T(8,128)(2,1)S(1)}, bf16[64,1024]{1,0:T(8,128)(2,1)}, u32[]{:S(2)}) copy-start(bf16[64,1024]{1,0:T(8,128)(2,1)} %param.16) | copy-start | bytes 393220
  302.2 232.9 %copy-start.5 = (f32[1024]{0:T(1024)S(1)}, f32[1024]{0:T(1024)}, u32[]{:S(2)}) copy-start(f32[1024]{0:T(1024)} %param.24) | copy-start | bytes 12292
  302.3 232.9 %copy-start.6 = (f32[1024]{0:T(1024)S(1)}, f32[1024]{0:T(1024)}, u32[]{:S(2)}) copy-start(f32[1024]{0:T(1024)} %param.23) | copy-start | bytes 12292
  302.3 232.9 %copy-start.7 = (f32[1024]{0:T(1024)S(1)}, f32[1024]{0:T(1024)}, u32[]{:S(2)}) copy-start(f32[1024]{0:T(1024)} %param.22) | copy-start | bytes 12292
  303.3 30.7 %all-to-all-start.1 = ((bf16[8,64,128]{2,1,0:T(8,128)(2,1)}), bf16[8,64,128]{2,1,0:T(8,128)(2,1)S(1)}, u32[]{:S(2)}, u32[]{:S(2)}) async-start(bf16[8,64,128]{2,1,0:T(8,128)(2,1)} %copy.35), calls=%async_computation.1 | async-start | bytes 262144 | tf_op jit(solution)/shard_map/all_to_all | solution.py:114
  535.1 11.4 %copy-start.2 = (f32[1024]{0:T(1024)S(1)}, f32[1024]{0:T(1024)}, u32[]{:S(2)}) copy-start(f32[1024]{0:T(1024)} %param.26) | copy-start | bytes 12292
  535.1 11.4 %copy-start.3 = (f32[1024]{0:T(1024)S(1)}, f32[1024]{0:T(1024)}, u32[]{:S(2)}) copy-start(f32[1024]{0:T(1024)} %param.25) | copy-start | bytes 12292
Sparse Core Ops, SparseCore 0:
  9.1 53.9 all-gather.5
  64.9 94.4 all-gather.7
  161.2 196.4 all-gather.11
  359.3 175.7 all-gather.9

commit v2 on v1

--- a/solution.py
+++ b/solution.py
@@ -91,9 +91,6 @@
     fresh_values = heads_qkv[:, 2 * width_here :].reshape(local_shape)
 
     full_out = lax.all_gather(w_out, "tp", axis=0, tiled=True)
-    full_up = lax.all_gather(w_up, "tp", axis=1, tiled=True)
-    full_b_up = lax.all_gather(b_up, "tp", axis=0, tiled=True)
-    full_down = lax.all_gather(w_down, "tp", axis=0, tiled=True)
 
     fresh_count = span_len[where_req]
     cached_count = cache_len[where_req]
@@ -115,11 +112,19 @@
 
     projected = jnp.dot(attention, full_out, preferred_element_type=jnp.float32)
     normed = layer_norm(tokens.astype(jnp.float32) + projected, ln1_gain, ln1_bias).astype(jnp.bfloat16)
+    n_tp = lax.axis_size("tp")
+    span_normed = lax.all_to_all(
+        jnp.broadcast_to(normed[None], (n_tp,) + normed.shape), "tp", split_axis=0, concat_axis=0, tiled=True
+    ).reshape(-1, normed.shape[1])
     hidden = jax.nn.gelu(
-        jnp.dot(normed, full_up, preferred_element_type=jnp.float32) + full_b_up,
+        jnp.dot(span_normed, w_up, preferred_element_type=jnp.float32) + b_up,
         approximate=False,
     ).astype(jnp.bfloat16)
-    summed = jnp.dot(hidden, full_down, preferred_element_type=jnp.float32) + b_down + normed.astype(jnp.float32)
+    partial = jnp.dot(hidden, w_down, preferred_element_type=jnp.float32).astype(jnp.bfloat16)
+    partial = lax.all_to_all(
+        partial.reshape((n_tp, -1) + partial.shape[1:]), "tp", split_axis=0, concat_axis=0, tiled=True
+    )
+    summed = jnp.sum(partial.astype(jnp.float32), axis=0) + b_down + normed.astype(jnp.float32)
     return layer_norm(summed, ln2_gain, ln2_bias).astype(jnp.bfloat16)
 
 

time: 561 us -> 365 us (0.65)
  waiting for transfers between devices: 380 us -> 186 us
  matrix products: 55.5 us -> 48.9 us
    all_gather x2 -> x0, waiting for transfers between devices: 199 us -> none  [the longest x1 177 us: shards(): full_up = lax.all_gather(w_up, 'tp', axis=1, tiled=True)]
    all_to_all x1, waiting for transfers between devices: 150 us -> 112 us  [shards(): lax.all_to_all(kv_cache, 'req', split_axis=1, concat_axis=1, tiled=True)]
    all_gather x1, waiting for transfers between devices: 28.4 us -> 65.8 us  [shards(): span_rows = lax.all_gather(tokens, 'tp', axis=0, tiled=True)]
    all_to_all x0 -> x2, blocking collectives: none -> 31.8 us  [the longest x1 16.4 us: shards(): lax.all_to_all(jnp.broadcast_to(normed[None], (n_tp,) + normed.shape), 't...]
    all_gather x1 -> x0, blocking collectives: 26.2 us -> none  [shards(): full_b_up = lax.all_gather(b_up, 'tp', axis=0, tiled=True)]
    dot_general x1, matrix products: 11.1 us -> 4.63 us  [shards(): jnp.dot(hidden, w_down, preferred_element_type=jnp.float32)]
    all_to_all x1, waiting for transfers between devices: 0.01 us -> 6.39 us  [shards(): lax.all_to_all(attention, 'tp', split_axis=0, concat_axis=1, tiled=True)]
    unnamed x22 -> x24, local copies, waits for them, and re-layouts: 12.3 us -> 12.4 us
  transfers between devices with their start and end apart: 6 -> 4, of which waited for: 4 -> 3; matrix products, arithmetic and copies ran while one was open for 19% -> 25% of each run, Pallas kernels for 0% -> 0%
where the time goes in v2:
time: 365 us; the launch traced here: 360 us
  waiting for transfers between devices  186 us (51%)
  matrix products  48.9 us (13%)
  other arithmetic  34.1 us (9%)
  blocking collectives  31.8 us (9%)
  local copies, waits for them, and re-layouts  29.6 us (8%)
  starting transfers between devices  16.2 us (4%)
  between operations  13.7 us (4%)
    all_to_all x1, waiting for transfers between devices, shards(): lax.all_to_all(kv_cache, 'req', split_axis=1, concat_axis=1, tiled=True)  112 us
    all_gather x1, waiting for transfers between devices, shards(): span_rows = lax.all_gather(tokens, 'tp', axis=0, tiled=True)  65.8 us
    dot_general x9, matrix products, partial_attention(): jnp.einsum('chd,nhd->hcn', queries, key_rows, preferred_element_type=jnp....  24.5 us
    reduce_sum x9, other arithmetic, partial_attention(): weight_sums = jnp.sum(weights.astype(jnp.float32), axis=-1)  21.2 us
    all_to_all x1, blocking collectives, shards(): lax.all_to_all(jnp.broadcast_to(normed[None], (n_tp,) + normed.shape), 't...  16.4 us
    dot_general x9, matrix products, partial_attention(): jnp.einsum('hcn,nhd->chd', weights, value_rows, preferred_element_type=jn...  15.8 us
    all_to_all x1, blocking collectives, shards(): lax.all_to_all(partial.reshape((n_tp, -1) + partial.shape[1:]), 'tp', spl...  15.4 us
    unnamed x24, local copies, waits for them, and re-layouts  12.4 us
  transfers between devices with their start and end apart: 4, of which 3 were waited for; matrix products, arithmetic and copies ran while one was open for 25% of the time, Pallas kernels for 0%

profile of v2, /device:TPU:80, one launch (start us, length us, event | category | flops | bytes accessed | tf_op | source)
XLA Modules:
  0.0 360.2 jit_solution(2658030651955312103)
XLA Ops:
  6.5 12.1 %copy.29 = bf16[2,32,512,128]{2,3,0,1:T(8,128)(2,1)} copy(bf16[2,32,512,128]{3,2,1,0:T(8,128)(2,1)} %param.27) | data formatting | bytes 16777216 | tf_op args[11]
  18.6 10.9 %all-to-all-start = ((bf16[2,32,512,128]{2,3,0,1:T(8,128)(2,1)}), bf16[2,32,512,128]{2,3,0,1:T(8,128)(2,1)}, u32[]{:S(2)}, u32[]{:S(2)}) async-start(bf16[2,32,512,128]{2,3,0,1:T(8,128)(2,1)} %copy.29), calls=%async_computation | async-start | bytes 16777216 | tf_op jit(solution)/shard_map/all_to_all | solution.py:82
  33.3 65.8 %all-gather.3.cloned.1.call-done = bf16[512,1024]{1,0:T(8,128)(2,1)} async-done(((bf16[64,1024]{1,0:T(8,128)(2,1)}), bf16[512,1024]{1,0:T(8,128)(2,1)}) %all-gather.3.cloned.1.call-update) | async-done | bytes 1048592 | tf_op jit(solution)/shard_map/all_gather | solution.py:84
  103.0 112.1 %all-to-all-done = bf16[2,32,512,128]{2,3,0,1:T(8,128)(2,1)} async-done(((bf16[2,32,512,128]{2,3,0,1:T(8,128)(2,1)}), bf16[2,32,512,128]{2,3,0,1:T(8,128)(2,1)}, u32[]{:S(2)}, u32[]{:S(2)}) %all-to-all-start) | async-done | bytes 8388640 | tf_op jit(solution)/shard_map/all_to_all | solution.py:82
  215.1 5.9 %fusion.93 = (bf16[1,32,512,128]{2,3,0,1:T(8,128)(2,1)}, bf16[1,32,512,128]{2,3,0,1:T(8,128)(2,1)}) fusion(bf16[2,32,512,128]{2,3,0,1:T(8,128)(2,1)} %all-to-all-done), kind=kLoop, calls=%fused_computation.137 | loop fusion | bytes 16777216 | tf_op jit(solution)/shard_map/slice | solution.py:103
  221.0 74.6 %while.14 = (s32[]{:T(128)}, f32[8,4,512,2]{2,1,3,0:T(4,128)S(1)}, f32[8,4,512,2]{2,3,1,0:T(2,128)S(1)}, f32[8,4,512,128]{2,3,1,0:T(8,128)}, s32[8,4]{1,0:T(8,12...) while((s32[]{:T(128)}, f32[8,4,512,2]{2,1,3,0:T(4,128)S(1)}, ...), condition=%wide.region_4.5_spmd, body=%wide.region_1.4_spmd.sunk | while | flops 557838336 | bytes 29612216 | solution.py:55
  221.7 3.0 bitcast_reduce_fusion.2
  224.7 2.6 convert_reduce_fusion.4
  231.1 3.0 bitcast_reduce_fusion.2
  234.1 2.6 convert_reduce_fusion.4
  240.4 3.0 bitcast_reduce_fusion.2
  243.4 2.6 convert_reduce_fusion.4
  246.0 1.9 fusion.113
  249.7 3.0 bitcast_reduce_fusion.2
  252.7 2.6 convert_reduce_fusion.4
  255.3 1.9 fusion.113
  259.0 3.0 bitcast_reduce_fusion.2
  262.0 2.6 convert_reduce_fusion.4
  268.4 3.0 bitcast_reduce_fusion.2
  271.4 2.6 convert_reduce_fusion.4
  274.0 1.9 fusion.113
  277.7 3.0 bitcast_reduce_fusion.2
  280.7 2.6 convert_reduce_fusion.4
  287.0 3.0 bitcast_reduce_fusion.2
  290.0 2.6 convert_reduce_fusion.4
  295.9 4.1 %fusion.12 = f32[512,2,64]{0,2,1:T(8,128)S(1)} fusion(f32[32,512,2,64]{1,3,2,0:T(8,128)} %bitcast.103, f32[1,512,2,64]{1,3,2,0:T(8,128)S(1)} %convolution_bitcast_fusion, f32[33,512,2]{1,2,0:T(2,128)S(1)} %get-tuple-element.105), kind=kLoop, calls=%fused_computation.24 | loop fusion | flops 6422528 | bytes 9048064 | tf_op jit(solution)/shard_map/reduce_sum | solution.py:36
  301.1 5.2 %all-to-all-start.1 = ((bf16[8,64,128]{2,1,0:T(8,128)(2,1)}), bf16[8,64,128]{2,1,0:T(8,128)(2,1)S(1)}, u32[]{:S(2)}, u32[]{:S(2)}) async-start(bf16[8,64,128]{2,1,0:T(8,128)(2,1)} %copy.35), calls=%async_computation.1 | async-start | bytes 262144 | tf_op jit(solution)/shard_map/all_to_all | solution.py:111
  306.3 6.4 %all-to-all-done.1 = bf16[8,64,128]{2,1,0:T(8,128)(2,1)S(1)} async-done(((bf16[8,64,128]{2,1,0:T(8,128)(2,1)}), bf16[8,64,128]{2,1,0:T(8,128)(2,1)S(1)}, u32[]{:S(2)}, u32[]{:S(2)}) %all-to-all-start.1) | async-done | bytes 131104 | tf_op jit(solution)/shard_map/all_to_all | solution.py:111
  312.7 2.2 fusion.95
  315.4 16.4 %all_to_all.31 = bf16[8,64,1024]{2,1,0:T(8,128)(2,1)S(1)} all-to-all(bf16[8,64,1024]{2,1,0:T(8,128)(2,1)S(1)} %broadcast_in_dim.109), channel_id=1, replica_groups=mesh['req'=32,'tp'=8] {'tp'}, dimensions={0} | all-to-all | bytes 2097152 | tf_op jit(solution)/shard_map/all_to_all | solution.py:116
  331.8 4.6 %convolution_convert_fusion = bf16[512,1024]{1,0:T(8,128)(2,1)S(1)} fusion(bf16[512,1024]{1,0:T(8,128)(2,1)S(1)} %copy-done, bf16[512,1024]{1,0:T(8,128)(2,1)S(1)} %bitcast.107, bf16[1024,512]{1,0:T(8,128)(2,1)} %param.19, f32[512]{0:T(512)S(1)} %copy-done.8), kind=kOutput, calls=%fused_computation.31 | convolution fusion | flops 1091567616 | bytes 4196352 | tf_op jit(solution)/shard_map/dot_general | solution.py:123
  336.5 15.4 %all_to_all.32 = bf16[8,64,1024]{2,1,0:T(8,128)(2,1)S(1)} all-to-all(bf16[8,64,1024]{2,1,0:T(8,128)(2,1)S(1)} %bitcast.108), channel_id=1, replica_groups=mesh['req'=32,'tp'=8] {'tp'}, dimensions={0} | all-to-all | bytes 2097152 | tf_op jit(solution)/shard_map/all_to_all | solution.py:124
  (104 shorter events, 35.2 us)
Async XLA Ops:
  6.5 325.3 %copy-start = (bf16[512,1024]{1,0:T(8,128)(2,1)S(1)}, bf16[512,1024]{1,0:T(8,128)(2,1)}, u32[]{:S(2)}) copy-start(bf16[512,1024]{1,0:T(8,128)(2,1)} %param.21) | copy-start | bytes 3145732
  18.6 12.4 %copy-start.1 = (bf16[1024,3,128]{2,0,1:T(8,128)(2,1)S(1)}, bf16[1024,3,128]{2,0,1:T(8,128)(2,1)}, u32[]{:S(2)}) copy-start(bf16[1024,3,128]{2,0,1:T(8,128)(2,1)} %param.17) | copy-start | bytes 2359300
  18.6 12.7 %copy-start.9 = (s32[32]{0:T(128)S(1)}, s32[32]{0:T(128)}, u32[]{:S(2)}) copy-start(s32[32]{0:T(128)} %param.28) | copy-start | bytes 388
  18.6 13.4 %copy-start.10 = (s32[32]{0:T(128)S(1)}, s32[32]{0:T(128)}, u32[]{:S(2)}) copy-start(s32[32]{0:T(128)} %param.29) | copy-start | bytes 388
  18.6 196.5 %all-to-all-start = ((bf16[2,32,512,128]{2,3,0,1:T(8,128)(2,1)}), bf16[2,32,512,128]{2,3,0,1:T(8,128)(2,1)}, u32[]{:S(2)}, u32[]{:S(2)}) async-start(bf16[2,32,512,128]{2,3,0,1:T(8,128)(2,1)} %copy.29), calls=%async_computation | async-start | bytes 16777216 | tf_op jit(solution)/shard_map/all_to_all | solution.py:82
  29.5 69.7 %all-gather.3.cloned.1.call-start = ((), (), s32[]{:S(2)}) async-start(), calls=%async_computation.4 | async-start | bytes 1179648 | tf_op jit(solution)/shard_map/all_gather | solution.py:84
  30.2 276.1 %all-gather.5.cloned.1.call-start = ((), (), s32[]{:S(2)}) async-start(), calls=%async_computation.5 | async-start | bytes 2359296 | tf_op jit(solution)/shard_map/all_gather | solution.py:93
  295.9 16.8 %copy-start.2 = (bf16[64,1024]{1,0:T(8,128)(2,1)S(1)}, bf16[64,1024]{1,0:T(8,128)(2,1)}, u32[]{:S(2)}) copy-start(bf16[64,1024]{1,0:T(8,128)(2,1)} %param.16) | copy-start | bytes 393220
  300.0 15.1 %copy-start.3 = (f32[1024]{0:T(1024)S(1)}, f32[1024]{0:T(1024)}, u32[]{:S(2)}) copy-start(f32[1024]{0:T(1024)} %param.24) | copy-start | bytes 12292
  300.0 15.1 %copy-start.4 = (f32[1024]{0:T(1024)S(1)}, f32[1024]{0:T(1024)}, u32[]{:S(2)}) copy-start(f32[1024]{0:T(1024)} %param.23) | copy-start | bytes 12292
  300.0 31.8 %copy-start.8 = (f32[512]{0:T(512)S(1)}, f32[512]{0:T(512)}, u32[]{:S(2)}) copy-start(f32[512]{0:T(512)} %param.20) | copy-start | bytes 6148
  301.1 11.6 %all-to-all-start.1 = ((bf16[8,64,128]{2,1,0:T(8,128)(2,1)}), bf16[8,64,128]{2,1,0:T(8,128)(2,1)S(1)}, u32[]{:S(2)}, u32[]{:S(2)}) async-start(bf16[8,64,128]{2,1,0:T(8,128)(2,1)} %copy.35), calls=%async_computation.1 | async-start | bytes 262144 | tf_op jit(solution)/shard_map/all_to_all | solution.py:111
  331.8 20.2 %copy-start.5 = (f32[1024]{0:T(1024)S(1)}, f32[1024]{0:T(1024)}, u32[]{:S(2)}) copy-start(f32[1024]{0:T(1024)} %param.22) | copy-start | bytes 12292
  336.4 16.1 %copy-start.6 = (f32[1024]{0:T(1024)S(1)}, f32[1024]{0:T(1024)}, u32[]{:S(2)}) copy-start(f32[1024]{0:T(1024)} %param.26) | copy-start | bytes 12292
  336.4 16.1 %copy-start.7 = (f32[1024]{0:T(1024)S(1)}, f32[1024]{0:T(1024)}, u32[]{:S(2)}) copy-start(f32[1024]{0:T(1024)} %param.25) | copy-start | bytes 12292
Sparse Core Ops, SparseCore 0:
  32.1 67.0 all-gather.2
  101.0 100.9 all-gather.4

commit v3 on v2

--- a/solution.py
+++ b/solution.py
@@ -1,10 +1,11 @@
 import jax
 import jax.numpy as jnp
 from jax import lax
+from jax.experimental import pallas as pl
+from jax.experimental.pallas import tpu as pltpu
 from jax.sharding import PartitionSpec as P
 
 HEAD_DIM = 64
-BLOCK_GROUP = 4
 
 masked_score = -1e30
 
@@ -37,26 +38,72 @@
     return (jnp.squeeze(highest, axis=axis), sums_out, blend_out)
 
 
-def cache_partials(queries, keys, values, cached_count):
-    total_blocks, block_width = keys.shape[0], keys.shape[1]
-    group = BLOCK_GROUP if total_blocks % BLOCK_GROUP == 0 else 1
+def cache_kernel(count_ref, q_ref, k_ref, v_ref, acc_ref, peak_ref, sum_ref):
+    block = pl.program_id(0)
 
-    def single(one_keys, one_values, block):
-        places = block * block_width + jnp.arange(block_width, dtype=jnp.int32)
-        allowed = jnp.broadcast_to((places < cached_count)[None, :], (queries.shape[0], block_width))
-        return partial_attention(queries, one_keys, one_values, allowed)
+    @pl.when(block == 0)
+    def _():
+        acc_ref[...] = jnp.zeros_like(acc_ref)
+        peak_ref[...] = jnp.full_like(peak_ref, masked_score)
+        sum_ref[...] = jnp.zeros_like(sum_ref)
 
-    def grouped(items):
-        return jax.vmap(single)(*items)
+    width = k_ref.shape[1]
+    places = block * width + lax.broadcasted_iota(jnp.int32, (1, width), 1)
+    allowed = places < count_ref[0]
+    for head in range(peak_ref.shape[0]):
+        cols = slice(head * HEAD_DIM, (head + 1) * HEAD_DIM)
+        scores = lax.dot_general(
+            q_ref[:, cols], k_ref[0, :, cols], (((1,), (1,)), ((), ())), preferred_element_type=jnp.float32
+        ) * HEAD_DIM ** (-0.5)
+        scores = jnp.where(allowed, scores, masked_score)
+        peak = jnp.max(scores, axis=1, keepdims=True)
+        weights = jnp.where(allowed, jnp.exp(scores - peak), 0.0).astype(jnp.bfloat16)
+        weight_sum = jnp.sum(weights.astype(jnp.float32), axis=1, keepdims=True)
+        blend = jnp.dot(weights, v_ref[0, :, cols], preferred_element_type=jnp.float32)
+        old = peak_ref[head]
+        new = jnp.maximum(old, peak)
+        keep = jnp.exp(old - new)
+        take = jnp.exp(peak - new)
+        peak_ref[head] = new
+        sum_ref[head] = sum_ref[head] * keep + weight_sum * take
+        acc_ref[:, cols] = acc_ref[:, cols] * keep + blend * take
 
-    def regroup(member):
-        return member.reshape((total_blocks // group, group) + member.shape[1:])
 
-    results = lax.map(
-        grouped,
-        (regroup(keys), regroup(values), regroup(jnp.arange(total_blocks, dtype=jnp.int32))),
+def cache_partials(queries, own_keys, own_values, cached_count):
+    span, width = queries.shape
+    total_blocks, block_width = own_keys.shape[0], own_keys.shape[1]
+    heads = width // HEAD_DIM
+    grid_spec = pltpu.PrefetchScalarGridSpec(
+        num_scalar_prefetch=1,
+        grid=(total_blocks,),
+        in_specs=[
+            pl.BlockSpec((span, width), lambda b, c: (0, 0)),
+            pl.BlockSpec((1, block_width, width), lambda b, c: (b, 0, 0)),
+            pl.BlockSpec((1, block_width, width), lambda b, c: (b, 0, 0)),
+        ],
+        out_specs=[
+            pl.BlockSpec((span, width), lambda b, c: (0, 0)),
+            pl.BlockSpec((heads, span, 1), lambda b, c: (0, 0, 0)),
+            pl.BlockSpec((heads, span, 1), lambda b, c: (0, 0, 0)),
+        ],
     )
-    return tuple(member.reshape((total_blocks,) + member.shape[2:]) for member in results)
+    flops = 4 * span * block_width * width * total_blocks
+    acc, peaks, sums = pl.pallas_call(
+        cache_kernel,
+        grid_spec=grid_spec,
+        out_shape=[
+            jax.ShapeDtypeStruct((span, width), jnp.float32),
+            jax.ShapeDtypeStruct((heads, span, 1), jnp.float32),
+            jax.ShapeDtypeStruct((heads, span, 1), jnp.float32),
+        ],
+        compiler_params=pltpu.CompilerParams(dimension_semantics=("arbitrary",)),
+        cost_estimate=pl.CostEstimate(
+            flops=flops,
+            transcendentals=heads * span * block_width * total_blocks,
+            bytes_accessed=own_keys.size * 4 + span * width * 6,
+        ),
+    )(jnp.reshape(cached_count, (1,)), queries, own_keys, own_values)
+    return peaks[..., 0].T, sums[..., 0].T, acc
 
 
 def shards(
@@ -79,7 +126,8 @@
     heads_here = width_here // HEAD_DIM
     where_req = lax.axis_index("req")
 
-    own_cache = lax.all_to_all(kv_cache, "req", split_axis=1, concat_axis=1, tiled=True)
+    own_keys = lax.all_to_all(kv_cache[0], "req", split_axis=0, concat_axis=0, tiled=True)
+    own_values = lax.all_to_all(kv_cache[1], "req", split_axis=0, concat_axis=0, tiled=True)
 
     span_rows = lax.all_gather(tokens, "tp", axis=0, tiled=True)
     flat_qkv = w_qkv.reshape(w_qkv.shape[0], 3 * width_here)
@@ -98,13 +146,11 @@
     allowed = (positions[None, :] <= positions[:, None]) & (positions[None, :] < fresh_count)
     fresh = partial_attention(queries, fresh_keys, fresh_values, allowed)
 
-    total_blocks, block_width = own_cache.shape[1], own_cache.shape[2]
-    cached = own_cache.reshape(2, total_blocks, block_width, heads_here, HEAD_DIM)
-    peaks, weight_sums, blended = cache_partials(queries, cached[0], cached[1], cached_count)
+    peaks, weight_sums, blended = cache_partials(heads_qkv[:, :width_here], own_keys, own_values, cached_count)
     peaks, weight_sums, blended = merge_axis(
-        jnp.concatenate([fresh[0][None], peaks]),
-        jnp.concatenate([fresh[1][None], weight_sums]),
-        jnp.concatenate([fresh[2][None], blended]),
+        jnp.stack([fresh[0], peaks]),
+        jnp.stack([fresh[1], weight_sums]),
+        jnp.stack([fresh[2], blended]),
         0,
     )
     attention = (blended / jnp.repeat(weight_sums, HEAD_DIM, axis=-1)).astype(jnp.bfloat16)

time: 365 us -> 375 us (1.027)
  blocking collectives: 31.8 us -> 137 us
  waiting for transfers between devices: 186 us -> 93.8 us
  Pallas kernels: 0 us -> 89.3 us
  matrix products: 48.9 us -> 10.2 us
  other arithmetic: 34.1 us -> 5.79 us
  local copies, waits for them, and re-layouts: 29.6 us -> 9.47 us
    all_to_all x0 -> x1, blocking collectives: none -> 104 us  [shards(): lax.all_to_all(kv_cache[0], 'req', split_axis=0, concat_axis=0, tiled=True)]
    pallas_call x0 -> x1, Pallas kernels: none -> 89.3 us  [cache_partials(): pl.pallas_call(cache_kernel, grid_spec=grid_spec, out_shape=[jax.ShapeDty...]
    all_to_all x1, waiting for transfers between devices: 112 us -> 31.3 us  [shards(): lax.all_to_all(kv_cache[1], 'req', split_axis=0, concat_axis=0, tiled=True)]
    dot_general x9 -> x1, matrix products: 24.5 us -> 0.62 us  [partial_attention(): jnp.einsum('chd,nhd->hcn', queries, key_rows, preferred_element_type=jnp....]
    reduce_sum x9 -> x1, other arithmetic: 21.2 us -> 0.57 us  [partial_attention(): weight_sums = jnp.sum(weights.astype(jnp.float32), axis=-1)]
    dot_general x9 -> x1, matrix products: 15.8 us -> 0.78 us  [partial_attention(): jnp.einsum('hcn,nhd->chd', weights, value_rows, preferred_element_type=jn...]
    unnamed x24 -> x25, local copies, waits for them, and re-layouts: 12.4 us -> 0.34 us
    all_gather x1, waiting for transfers between devices: 65.8 us -> 54.7 us  [shards(): span_rows = lax.all_gather(tokens, 'tp', axis=0, tiled=True)]
  transfers between devices with their start and end apart: 4 -> 4, of which waited for: 3 -> 3; matrix products, arithmetic and copies ran while one was open for 25% -> 3% of each run, Pallas kernels for 0% -> 24%
where the time goes in v3:
time: 375 us; the launch traced here: 372 us
  blocking collectives  137 us (37%)
  waiting for transfers between devices  93.8 us (25%)
  Pallas kernels  89.3 us (24%)
  between operations  13.7 us (4%)
  starting transfers between devices  13.2 us (4%)
  matrix products  10.2 us (3%)
  local copies, waits for them, and re-layouts  9.47 us (3%)
  other arithmetic  5.79 us (2%)
    all_to_all x1, blocking collectives, shards(): lax.all_to_all(kv_cache[0], 'req', split_axis=0, concat_axis=0, tiled=True)  104 us
    pallas_call x1, Pallas kernels, cache_partials(): pl.pallas_call(cache_kernel, grid_spec=grid_spec, out_shape=[jax.ShapeDty...  89.3 us
    all_gather x1, waiting for transfers between devices, shards(): span_rows = lax.all_gather(tokens, 'tp', axis=0, tiled=True)  54.7 us
    all_to_all x1, waiting for transfers between devices, shards(): lax.all_to_all(kv_cache[1], 'req', split_axis=0, concat_axis=0, tiled=True)  31.3 us
    all_to_all x1, blocking collectives, shards(): lax.all_to_all(jnp.broadcast_to(normed[None], (n_tp,) + normed.shape), 't...  16.4 us
    all_to_all x1, blocking collectives, shards(): lax.all_to_all(partial.reshape((n_tp, -1) + partial.shape[1:]), 'tp', spl...  15.8 us
    all_to_all x1, starting transfers between devices, shards(): lax.all_to_all(kv_cache[1], 'req', split_axis=0, concat_axis=0, tiled=True)  7.6 us
  transfers between devices with their start and end apart: 4, of which 3 were waited for; matrix products, arithmetic and copies ran while one was open for 3% of the time, Pallas kernels for 24%

profile of v3, /device:TPU:80, one launch (start us, length us, event | category | flops | bytes accessed | tf_op | source)
XLA Modules:
  0.0 372.2 jit_solution(16614130568943945677)
XLA Ops:
  6.5 5.3 %slice_bitcast_fusion = (bf16[32,512,128]{2,1,0:T(8,128)(2,1)}, bf16[32,512,128]{2,1,0:T(8,128)(2,1)S(1)}) fusion(bf16[2,32,512,128]{3,2,1,0:T(8,128)(2,1)} %param.25), kind=kLoop, calls=%fused_computation | loop fusion | bytes 16777216 | tf_op jit(solution)/shard_map/squeeze | solution.py:130
  11.8 104.5 %all_to_all.36.k_ref = bf16[32,512,128]{2,1,0:T(8,128)(2,1)} all-to-all(bf16[32,512,128]{2,1,0:T(8,128)(2,1)S(1)} %get-tuple-element.14), channel_id=1, replica_groups=mesh['req'=32,'tp'=8] {'req'}, dimensions={0} | all-to-all | bytes 8388608 | tf_op jit(solution)/shard_map/all_to_all | solution.py:129
  116.3 7.6 %all-to-all-start.1 = ((bf16[32,512,128]{2,1,0:T(8,128)(2,1)}), bf16[32,512,128]{2,1,0:T(8,128)(2,1)}, u32[]{:S(2)}, u32[]{:S(2)}) async-start(bf16[32,512,128]{2,1,0:T(8,128)(2,1)} %get-tuple-element.13), calls=%async_computation.1 | async-start | bytes 8388608 | tf_op jit(solution)/shard_map/all_to_all | solution.py:130
  124.0 0.7 all-gather.3.cloned.1.call-update
  124.7 0.7 all-gather.5.cloned.1.call-update
  125.4 0.3 copy.29
  125.7 0.6 dynamic_slice.7.count_ref
  126.3 0.6 dynamic_slice.6
  126.9 0.6 iota_compare_fusion.1
  127.7 54.7 %all-gather.3.cloned.1.call-done = bf16[512,1024]{1,0:T(8,128)(2,1)} async-done(((bf16[64,1024]{1,0:T(8,128)(2,1)}), bf16[512,1024]{1,0:T(8,128)(2,1)}) %all-gather.3.cloned.1.call-update) | async-done | bytes 1048592 | tf_op jit(solution)/shard_map/all_gather | solution.py:132
  182.4 2.0 convolution_convert_fusion.1
  184.8 0.6 fusion
  185.5 0.8 convolution_bitcast_fusion
  186.2 0.6 convert_reduce_fusion.1
  186.8 31.3 %all-to-all-done.1.v_ref = bf16[32,512,128]{2,1,0:T(8,128)(2,1)} async-done(((bf16[32,512,128]{2,1,0:T(8,128)(2,1)}), bf16[32,512,128]{2,1,0:T(8,128)(2,1)}, u32[]{:S(2)}, u32[]{:S(2)}) %all-to-all-start.1) | async-done | bytes 4194336 | tf_op jit(solution)/shard_map/all_to_all | solution.py:130
  218.2 89.3 %shard_map.136 = (f32[512,128]{1,0:T(8,128)}, f32[2,512,1]{2,1,0:T(8,128)}, f32[2,512,1]{2,1,0:T(8,128)}) custom-call(s32[1]{0:T(128)} %dynamic_slice.7.count_ref, bf16[512,128]{1,0:T(8,128)(2,1)} %copy-done.3, bf16[32,512,128]{2,1,0:T(8,128)(2,1)} %all_to_all.36.k_ref, bf16[32,512,128]{2,1,0:T(8,128)(2,1)} %all-to-all-done.1.v_ref), custom_call_target="tpu_custom_call" | custom-call | flops 4294967296 | bytes 8781824 | tf_op jit(solution)/shard_map/pallas_call | solution.py:91
  307.5 1.1 copy.35
  308.6 1.3 reduce.4
  309.9 1.3 reduce.3
  311.3 0.2 convert_element_type.42
  311.5 0.8 copy.36
  312.3 5.6 %all-to-all-start.2 = ((bf16[8,64,128]{2,1,0:T(8,128)(2,1)}), bf16[8,64,128]{2,1,0:T(8,128)(2,1)S(1)}, u32[]{:S(2)}, u32[]{:S(2)}) async-start(bf16[8,64,128]{2,1,0:T(8,128)(2,1)} %copy.36), calls=%async_computation.2 | async-start | bytes 262144 | tf_op jit(solution)/shard_map/all_to_all | solution.py:157
  317.9 6.4 %all-to-all-done.2 = bf16[8,64,128]{2,1,0:T(8,128)(2,1)S(1)} async-done(((bf16[8,64,128]{2,1,0:T(8,128)(2,1)}), bf16[8,64,128]{2,1,0:T(8,128)(2,1)S(1)}, u32[]{:S(2)}, u32[]{:S(2)}) %all-to-all-start.2) | async-done | bytes 131104 | tf_op jit(solution)/shard_map/all_to_all | solution.py:157
  324.3 2.2 fusion.81
  326.5 0.2 multiply_reduce_fusion.1
  327.0 16.4 %all_to_all.37 = bf16[8,64,1024]{2,1,0:T(8,128)(2,1)S(1)} all-to-all(bf16[8,64,1024]{2,1,0:T(8,128)(2,1)S(1)} %broadcast_in_dim.29), channel_id=1, replica_groups=mesh['req'=32,'tp'=8] {'tp'}, dimensions={0} | all-to-all | bytes 2097152 | tf_op jit(solution)/shard_map/all_to_all | solution.py:162
  343.4 4.6 %convolution_convert_fusion = bf16[512,1024]{1,0:T(8,128)(2,1)S(1)} fusion(bf16[512,1024]{1,0:T(8,128)(2,1)S(1)} %copy-done, bf16[512,1024]{1,0:T(8,128)(2,1)S(1)} %bitcast.52, bf16[1024,512]{1,0:T(8,128)(2,1)} %param.17, f32[512]{0:T(512)S(1)} %copy-done.9), kind=kOutput, calls=%fused_computation.8 | convolution fusion | flops 1091567616 | bytes 4196352 | tf_op jit(solution)/shard_map/dot_general | solution.py:169
  348.1 15.8 %all_to_all.38 = bf16[8,64,1024]{2,1,0:T(8,128)(2,1)S(1)} all-to-all(bf16[8,64,1024]{2,1,0:T(8,128)(2,1)S(1)} %bitcast.53), channel_id=1, replica_groups=mesh['req'=32,'tp'=8] {'tp'}, dimensions={0} | all-to-all | bytes 2097152 | tf_op jit(solution)/shard_map/all_to_all | solution.py:170
  363.9 0.2 convert_reduce_fusion
  364.1 0.2 fusion.46
  364.3 0.2 multiply_reduce_fusion
  364.6 0.8 add_convert_fusion
  (42 shorter events, 1.1 us)
Async XLA Ops:
  6.5 336.9 %copy-start = (bf16[512,1024]{1,0:T(8,128)(2,1)S(1)}, bf16[512,1024]{1,0:T(8,128)(2,1)}, u32[]{:S(2)}) copy-start(bf16[512,1024]{1,0:T(8,128)(2,1)} %param.19) | copy-start | bytes 3145732
  116.3 9.1 %copy-start.1 = (bf16[1024,3,128]{2,0,1:T(8,128)(2,1)S(1)}, bf16[1024,3,128]{2,0,1:T(8,128)(2,1)}, u32[]{:S(2)}) copy-start(bf16[1024,3,128]{2,0,1:T(8,128)(2,1)} %param.15) | copy-start | bytes 2359300
  116.3 9.4 %copy-start.10 = (s32[32]{0:T(128)S(1)}, s32[32]{0:T(128)}, u32[]{:S(2)}) copy-start(s32[32]{0:T(128)} %param.26) | copy-start | bytes 388
  116.3 10.0 %copy-start.11 = (s32[32]{0:T(128)S(1)}, s32[32]{0:T(128)}, u32[]{:S(2)}) copy-start(s32[32]{0:T(128)} %param.27) | copy-start | bytes 388
  116.3 101.9 %all-to-all-start.1 = ((bf16[32,512,128]{2,1,0:T(8,128)(2,1)}), bf16[32,512,128]{2,1,0:T(8,128)(2,1)}, u32[]{:S(2)}, u32[]{:S(2)}) async-start(bf16[32,512,128]{2,1,0:T(8,128)(2,1)} %get-tuple-element.13), calls=%async_computation.1 | async-start | bytes 8388608 | tf_op jit(solution)/shard_map/all_to_all | solution.py:130
  123.9 58.5 %all-gather.3.cloned.1.call-start = ((), (), s32[]{:S(2)}) async-start(), calls=%async_computation.5 | async-start | bytes 1179648 | tf_op jit(solution)/shard_map/all_gather | solution.py:132
  124.6 193.3 %all-gather.5.cloned.1.call-start = ((), (), s32[]{:S(2)}) async-start(), calls=%async_computation.6 | async-start | bytes 2359296 | tf_op jit(solution)/shard_map/all_gather | solution.py:141
  184.5 1.8 copy-start.3
  307.5 16.8 %copy-start.2 = (bf16[64,1024]{1,0:T(8,128)(2,1)S(1)}, bf16[64,1024]{1,0:T(8,128)(2,1)}, u32[]{:S(2)}) copy-start(bf16[64,1024]{1,0:T(8,128)(2,1)} %param.14) | copy-start | bytes 393220
  311.3 15.5 %copy-start.4 = (f32[1024]{0:T(1024)S(1)}, f32[1024]{0:T(1024)}, u32[]{:S(2)}) copy-start(f32[1024]{0:T(1024)} %param.22) | copy-start | bytes 12292
  311.3 15.5 %copy-start.5 = (f32[1024]{0:T(1024)S(1)}, f32[1024]{0:T(1024)}, u32[]{:S(2)}) copy-start(f32[1024]{0:T(1024)} %param.21) | copy-start | bytes 12292
  312.3 12.0 %all-to-all-start.2 = ((bf16[8,64,128]{2,1,0:T(8,128)(2,1)}), bf16[8,64,128]{2,1,0:T(8,128)(2,1)S(1)}, u32[]{:S(2)}, u32[]{:S(2)}) async-start(bf16[8,64,128]{2,1,0:T(8,128)(2,1)} %copy.36), calls=%async_computation.2 | async-start | bytes 262144 | tf_op jit(solution)/shard_map/all_to_all | solution.py:157
  326.5 16.9 %copy-start.9 = (f32[512]{0:T(512)S(1)}, f32[512]{0:T(512)}, u32[]{:S(2)}) copy-start(f32[512]{0:T(512)} %param.18) | copy-start | bytes 6148
  348.1 16.0 %copy-start.6 = (f32[1024]{0:T(1024)S(1)}, f32[1024]{0:T(1024)}, u32[]{:S(2)}) copy-start(f32[1024]{0:T(1024)} %param.20) | copy-start | bytes 12292
  348.1 16.5 %copy-start.7 = (f32[1024]{0:T(1024)S(1)}, f32[1024]{0:T(1024)}, u32[]{:S(2)}) copy-start(f32[1024]{0:T(1024)} %param.24) | copy-start | bytes 12292
  348.1 16.5 %copy-start.8 = (f32[1024]{0:T(1024)S(1)}, f32[1024]{0:T(1024)}, u32[]{:S(2)}) copy-start(f32[1024]{0:T(1024)} %param.23) | copy-start | bytes 12292
Sparse Core Ops, SparseCore 0:
  126.5 55.8 all-gather.2
  184.2 63.9 all-gather.4

commit v4 on v3

--- a/solution.py
+++ b/solution.py
@@ -38,72 +38,89 @@
     return (jnp.squeeze(highest, axis=axis), sums_out, blend_out)
 
 
-def cache_kernel(count_ref, q_ref, k_ref, v_ref, acc_ref, peak_ref, sum_ref):
+def cache_kernel(count_ref, q_ref, kt_ref, v_ref, acc_ref, peak_ref):
     block = pl.program_id(0)
+    heads = q_ref.shape[0]
+    width = kt_ref.shape[2]
+    start = block * width
+    scale = HEAD_DIM ** (-0.5)
 
     @pl.when(block == 0)
     def _():
         acc_ref[...] = jnp.zeros_like(acc_ref)
         peak_ref[...] = jnp.full_like(peak_ref, masked_score)
-        sum_ref[...] = jnp.zeros_like(sum_ref)
-
-    width = k_ref.shape[1]
-    places = block * width + lax.broadcasted_iota(jnp.int32, (1, width), 1)
-    allowed = places < count_ref[0]
-    for head in range(peak_ref.shape[0]):
-        cols = slice(head * HEAD_DIM, (head + 1) * HEAD_DIM)
-        scores = lax.dot_general(
-            q_ref[:, cols], k_ref[0, :, cols], (((1,), (1,)), ((), ())), preferred_element_type=jnp.float32
-        ) * HEAD_DIM ** (-0.5)
-        scores = jnp.where(allowed, scores, masked_score)
-        peak = jnp.max(scores, axis=1, keepdims=True)
-        weights = jnp.where(allowed, jnp.exp(scores - peak), 0.0).astype(jnp.bfloat16)
-        weight_sum = jnp.sum(weights.astype(jnp.float32), axis=1, keepdims=True)
-        blend = jnp.dot(weights, v_ref[0, :, cols], preferred_element_type=jnp.float32)
-        old = peak_ref[head]
-        new = jnp.maximum(old, peak)
-        keep = jnp.exp(old - new)
-        take = jnp.exp(peak - new)
-        peak_ref[head] = new
-        sum_ref[head] = sum_ref[head] * keep + weight_sum * take
-        acc_ref[:, cols] = acc_ref[:, cols] * keep + blend * take
-
-
-def cache_partials(queries, own_keys, own_values, cached_count):
+
+    def step(masked):
+        allowed = start + lax.broadcasted_iota(jnp.int32, (1, width), 1) < count_ref[0]
+        lane = lax.broadcasted_iota(jnp.int32, (1, v_ref.shape[2]), 1)
+        for head in range(heads):
+            raw = jnp.dot(
+                q_ref[head], kt_ref[0, head * HEAD_DIM : (head + 1) * HEAD_DIM, :], preferred_element_type=jnp.float32
+            )
+            if masked:
+                raw = jnp.where(allowed, raw, masked_score)
+            top = jnp.max(raw, axis=1, keepdims=True)
+            weights = jnp.exp((raw - top) * scale)
+            if masked:
+                weights = jnp.where(allowed, weights, 0.0)
+            weights = weights.astype(jnp.bfloat16)
+            own = (lane >= head * HEAD_DIM) & (lane < (head + 1) * HEAD_DIM)
+            values = jnp.where(own, v_ref[0], jnp.ones_like(v_ref[0]))
+            blend = jnp.dot(weights, values, preferred_element_type=jnp.float32)
+            peak = top * scale
+            old = peak_ref[head]
+            new = jnp.maximum(old, peak)
+            peak_ref[head] = new
+            acc_ref[head] = acc_ref[head] * jnp.exp(old - new) + blend * jnp.exp(peak - new)
+
+    full = start + width <= count_ref[0]
+    some = start < count_ref[0]
+
+    @pl.when(full)
+    def _():
+        step(False)
+
+    @pl.when(some & jnp.logical_not(full))
+    def _():
+        step(True)
+
+
+def cache_partials(queries, own_key_cols, own_values, cached_count):
     span, width = queries.shape
-    total_blocks, block_width = own_keys.shape[0], own_keys.shape[1]
+    total_blocks, block_width = own_values.shape[0], own_values.shape[1]
     heads = width // HEAD_DIM
+    per_head = queries.reshape(span, heads, HEAD_DIM).transpose(1, 0, 2)
     grid_spec = pltpu.PrefetchScalarGridSpec(
         num_scalar_prefetch=1,
         grid=(total_blocks,),
         in_specs=[
-            pl.BlockSpec((span, width), lambda b, c: (0, 0)),
-            pl.BlockSpec((1, block_width, width), lambda b, c: (b, 0, 0)),
+            pl.BlockSpec((heads, span, HEAD_DIM), lambda b, c: (0, 0, 0)),
+            pl.BlockSpec((1, width, block_width), lambda b, c: (b, 0, 0)),
             pl.BlockSpec((1, block_width, width), lambda b, c: (b, 0, 0)),
         ],
         out_specs=[
-            pl.BlockSpec((span, width), lambda b, c: (0, 0)),
-            pl.BlockSpec((heads, span, 1), lambda b, c: (0, 0, 0)),
+            pl.BlockSpec((heads, span, width), lambda b, c: (0, 0, 0)),
             pl.BlockSpec((heads, span, 1), lambda b, c: (0, 0, 0)),
         ],
     )
-    flops = 4 * span * block_width * width * total_blocks
-    acc, peaks, sums = pl.pallas_call(
+    acc, peaks = pl.pallas_call(
         cache_kernel,
         grid_spec=grid_spec,
         out_shape=[
-            jax.ShapeDtypeStruct((span, width), jnp.float32),
-            jax.ShapeDtypeStruct((heads, span, 1), jnp.float32),
+            jax.ShapeDtypeStruct((heads, span, width), jnp.float32),
             jax.ShapeDtypeStruct((heads, span, 1), jnp.float32),
         ],
         compiler_params=pltpu.CompilerParams(dimension_semantics=("arbitrary",)),
         cost_estimate=pl.CostEstimate(
-            flops=flops,
+            flops=2 * span * block_width * (HEAD_DIM + width) * heads * total_blocks,
             transcendentals=heads * span * block_width * total_blocks,
-            bytes_accessed=own_keys.size * 4 + span * width * 6,
+            bytes_accessed=own_values.size * 4 + span * width * 2 + heads * span * width * 4,
         ),
-    )(jnp.reshape(cached_count, (1,)), queries, own_keys, own_values)
-    return peaks[..., 0].T, sums[..., 0].T, acc
+    )(jnp.reshape(cached_count, (1,)), per_head, own_key_cols, own_values)
+    spare = [((head + 1) % heads) * HEAD_DIM for head in range(heads)]
+    blended = jnp.concatenate([acc[head, :, head * HEAD_DIM : (head + 1) * HEAD_DIM] for head in range(heads)], axis=1)
+    sums = jnp.stack([acc[head, :, spare[head]] for head in range(heads)], axis=1)
+    return peaks[..., 0].T, sums, blended
 
 
 def shards(
@@ -126,7 +143,7 @@
     heads_here = width_here // HEAD_DIM
     where_req = lax.axis_index("req")
 
-    own_keys = lax.all_to_all(kv_cache[0], "req", split_axis=0, concat_axis=0, tiled=True)
+    own_key_cols = lax.all_to_all(jnp.swapaxes(kv_cache[0], 1, 2), "req", split_axis=0, concat_axis=0, tiled=True)
     own_values = lax.all_to_all(kv_cache[1], "req", split_axis=0, concat_axis=0, tiled=True)
 
     span_rows = lax.all_gather(tokens, "tp", axis=0, tiled=True)
@@ -146,7 +163,7 @@
     allowed = (positions[None, :] <= positions[:, None]) & (positions[None, :] < fresh_count)
     fresh = partial_attention(queries, fresh_keys, fresh_values, allowed)
 
-    peaks, weight_sums, blended = cache_partials(heads_qkv[:, :width_here], own_keys, own_values, cached_count)
+    peaks, weight_sums, blended = cache_partials(heads_qkv[:, :width_here], own_key_cols, own_values, cached_count)
     peaks, weight_sums, blended = merge_axis(
         jnp.stack([fresh[0], peaks]),
         jnp.stack([fresh[1], weight_sums]),

time: 375 us -> 324 us (0.86)
  blocking collectives: 137 us -> 28 us
  waiting for transfers between devices: 93.8 us -> 182 us
  Pallas kernels: 89.3 us -> 45.2 us
  starting transfers between devices: 13.2 us -> 23.4 us
  local copies, waits for them, and re-layouts: 9.47 us -> 17.8 us
    all_to_all x1 -> x0, blocking collectives: 104 us -> none  [shards(): lax.all_to_all(kv_cache[0], 'req', split_axis=0, concat_axis=0, tiled=True)]
    all_to_all x1, waiting for transfers between devices: 31.3 us -> 88.2 us  [shards(): lax.all_to_all(kv_cache[1], 'req', split_axis=0, concat_axis=0, tiled=True)]
    pallas_call x1, Pallas kernels: 89.3 us -> 45.2 us  [cache_partials(): pl.pallas_call(cache_kernel, grid_spec=grid_spec, out_shape=[jax.ShapeDty...]
    all_to_all x0 -> x1, waiting for transfers between devices: none -> 31 us  [shards(): lax.all_to_all(jnp.swapaxes(kv_cache[0], 1, 2), 'req', split_axis=0, conc...]
    all_to_all x0 -> x1, starting transfers between devices: none -> 7.01 us  [shards(): lax.all_to_all(jnp.swapaxes(kv_cache[0], 1, 2), 'req', split_axis=0, conc...]
    unnamed x25 -> x28, local copies, waits for them, and re-layouts: 0.34 us -> 6.89 us
  transfers between devices with their start and end apart: 4 -> 5, of which waited for: 3 -> 4; matrix products, arithmetic and copies ran while one was open for 3% -> 5% of each run, Pallas kernels for 24% -> 14%
where the time goes in v4:
time: 324 us; the launch traced here: 323 us
  waiting for transfers between devices  182 us (56%)
  Pallas kernels  45.2 us (14%)
  blocking collectives  28 us (9%)
  starting transfers between devices  23.4 us (7%)
  local copies, waits for them, and re-layouts  17.8 us (5%)
  between operations  13.7 us (4%)
  matrix products  10 us (3%)
  other arithmetic  3.61 us (1%)
    all_to_all x1, waiting for transfers between devices, shards(): lax.all_to_all(kv_cache[1], 'req', split_axis=0, concat_axis=0, tiled=True)  88.2 us
    all_gather x1, waiting for transfers between devices, shards(): span_rows = lax.all_gather(tokens, 'tp', axis=0, tiled=True)  54.7 us
    pallas_call x1, Pallas kernels, cache_partials(): pl.pallas_call(cache_kernel, grid_spec=grid_spec, out_shape=[jax.ShapeDty...  45.2 us
    all_to_all x1, waiting for transfers between devices, shards(): lax.all_to_all(jnp.swapaxes(kv_cache[0], 1, 2), 'req', split_axis=0, conc...  31 us
    all_to_all x1, blocking collectives, shards(): lax.all_to_all(partial.reshape((n_tp, -1) + partial.shape[1:]), 'tp', spl...  14.2 us
    all_to_all x1, blocking collectives, shards(): lax.all_to_all(jnp.broadcast_to(normed[None], (n_tp,) + normed.shape), 't...  13.9 us
    all_to_all x1, starting transfers between devices, shards(): lax.all_to_all(kv_cache[1], 'req', split_axis=0, concat_axis=0, tiled=True)  10.7 us
    all_to_all x1, starting transfers between devices, shards(): lax.all_to_all(jnp.swapaxes(kv_cache[0], 1, 2), 'req', split_axis=0, conc...  7.01 us
  transfers between devices with their start and end apart: 5, of which 4 were waited for; matrix products, arithmetic and copies ran while one was open for 5% of the time, Pallas kernels for 14%

profile of v4, /device:TPU:80, one launch (start us, length us, event | category | flops | bytes accessed | tf_op | source)
XLA Modules:
  0.0 323.4 jit_solution(9996582323806588981)
XLA Ops:
  6.5 6.0 %slice_bitcast_fusion = (bf16[32,512,128]{2,1,0:T(8,128)(2,1)}, bf16[1,32,512,128]{3,2,1,0:T(8,128)(2,1)}) fusion(bf16[2,32,512,128]{3,2,1,0:T(8,128)(2,1)} %param.25), kind=kLoop, calls=%fused_computation | loop fusion | bytes 16777216 | tf_op jit(solution)/shard_map/squeeze | solution.py:147
  12.5 10.7 %all-to-all-start.1 = ((bf16[32,512,128]{2,1,0:T(8,128)(2,1)}), bf16[32,512,128]{2,1,0:T(8,128)(2,1)}, u32[]{:S(2)}, u32[]{:S(2)}) async-start(bf16[32,512,128]{2,1,0:T(8,128)(2,1)} %get-tuple-element.13), calls=%async_computation.1 | async-start | bytes 8388608 | tf_op jit(solution)/shard_map/all_to_all | solution.py:147
  23.3 6.5 %copy.33 = bf16[1,32,512,128]{2,3,1,0:T(8,128)(2,1)} copy(bf16[1,32,512,128]{3,2,1,0:T(8,128)(2,1)} %get-tuple-element.14) | data formatting | bytes 8388608
  29.8 88.2 %all-to-all-done.1.v_ref = bf16[32,512,128]{2,1,0:T(8,128)(2,1)} async-done(((bf16[32,512,128]{2,1,0:T(8,128)(2,1)}), bf16[32,512,128]{2,1,0:T(8,128)(2,1)}, u32[]{:S(2)}, u32[]{:S(2)}) %all-to-all-start.1) | async-done | bytes 4194336 | tf_op jit(solution)/shard_map/all_to_all | solution.py:147
  118.0 7.0 %all-to-all-start = ((bf16[32,128,512]{2,1,0:T(8,128)(2,1)}), bf16[32,128,512]{2,1,0:T(8,128)(2,1)}, u32[]{:S(2)}, u32[]{:S(2)}) async-start(bf16[32,128,512]{2,1,0:T(8,128)(2,1)} %bitcast.58), calls=%async_computation | async-start | bytes 8388608 | tf_op jit(solution)/shard_map/all_to_all | solution.py:146
  125.0 0.7 all-gather.3.cloned.1.call-update
  125.8 0.7 all-gather.5.cloned.1.call-update
  126.5 0.6 dynamic_slice.6
  127.1 0.6 dynamic_slice.7.count_ref
  127.7 0.3 copy.25
  128.0 0.6 iota_compare_fusion.1
  128.8 54.7 %all-gather.3.cloned.1.call-done = bf16[512,1024]{1,0:T(8,128)(2,1)} async-done(((bf16[64,1024]{1,0:T(8,128)(2,1)}), bf16[512,1024]{1,0:T(8,128)(2,1)}) %all-gather.3.cloned.1.call-update) | async-done | bytes 1048592 | tf_op jit(solution)/shard_map/all_gather | solution.py:149
  183.5 1.8 convolution_convert_fusion.1
  185.4 0.8 copy.26
  186.2 0.6 fusion
  186.8 0.8 convolution_bitcast_fusion
  187.6 0.6 convert_reduce_fusion.1
  188.2 31.0 %all-to-all-done.kt_ref = bf16[32,128,512]{2,1,0:T(8,128)(2,1)} async-done(((bf16[32,128,512]{2,1,0:T(8,128)(2,1)}), bf16[32,128,512]{2,1,0:T(8,128)(2,1)}, u32[]{:S(2)}, u32[]{:S(2)}) %all-to-all-start) | async-done | bytes 4194336 | tf_op jit(solution)/shard_map/all_to_all | solution.py:146
  219.2 45.2 %shard_map.136 = (f32[2,512,128]{2,1,0:T(8,128)}, f32[2,512,1]{2,1,0:T(8,128)}) custom-call(s32[1]{0:T(128)} %dynamic_slice.7.count_ref, bf16[2,512,64]{2,1,0:T(8,128)(2,1)} %bitcast.65, bf16[32,128,512]{2,1,0:T(8,128)(2,1)} %all-to-all-done.kt_ref, bf16[32,512,128]{2,1,0:T(8,128)(2,1)} %all-to-all-done.1.v_ref), custom_call_target="tpu_custom_call" | custom-call | flops 6442450944 | bytes 9043968 | tf_op jit(solution)/shard_map/pallas_call | solution.py:106
  264.4 1.2 slice_bitcast_fusion.2
  266.0 0.2 reduce.3
  266.2 0.3 slice_reduce_fusion.1
  266.9 0.8 copy.30
  267.7 5.5 %all-to-all-start.2 = ((bf16[8,64,128]{2,1,0:T(8,128)(2,1)}), bf16[8,64,128]{2,1,0:T(8,128)(2,1)S(1)}, u32[]{:S(2)}, u32[]{:S(2)}) async-start(bf16[8,64,128]{2,1,0:T(8,128)(2,1)} %copy.30), calls=%async_computation.2 | async-start | bytes 262144 | tf_op jit(solution)/shard_map/all_to_all | solution.py:174
  273.3 6.4 %all-to-all-done.2 = bf16[8,64,128]{2,1,0:T(8,128)(2,1)S(1)} async-done(((bf16[8,64,128]{2,1,0:T(8,128)(2,1)}), bf16[8,64,128]{2,1,0:T(8,128)(2,1)S(1)}, u32[]{:S(2)}, u32[]{:S(2)}) %all-to-all-start.2) | async-done | bytes 131104 | tf_op jit(solution)/shard_map/all_to_all | solution.py:174
  279.7 2.2 fusion.81
  282.3 13.9 %all_to_all.36 = bf16[8,64,1024]{2,1,0:T(8,128)(2,1)S(1)} all-to-all(bf16[8,64,1024]{2,1,0:T(8,128)(2,1)S(1)} %broadcast_in_dim.29), channel_id=1, replica_groups=mesh['req'=32,'tp'=8] {'tp'}, dimensions={0} | all-to-all | bytes 2097152 | tf_op jit(solution)/shard_map/all_to_all | solution.py:179
  296.2 4.6 %convolution_convert_fusion = bf16[512,1024]{1,0:T(8,128)(2,1)S(1)} fusion(bf16[512,1024]{1,0:T(8,128)(2,1)S(1)} %copy-done, bf16[512,1024]{1,0:T(8,128)(2,1)S(1)} %bitcast.60, bf16[1024,512]{1,0:T(8,128)(2,1)} %param.17, f32[512]{0:T(512)S(1)} %copy-done.10), kind=kOutput, calls=%fused_computation.7 | convolution fusion | flops 1091567616 | bytes 4196352 | tf_op jit(solution)/shard_map/dot_general | solution.py:186
  300.9 14.2 %all_to_all.37 = bf16[8,64,1024]{2,1,0:T(8,128)(2,1)S(1)} all-to-all(bf16[8,64,1024]{2,1,0:T(8,128)(2,1)S(1)} %bitcast.61), channel_id=1, replica_groups=mesh['req'=32,'tp'=8] {'tp'}, dimensions={0} | all-to-all | bytes 2097152 | tf_op jit(solution)/shard_map/all_to_all | solution.py:187
  315.2 0.2 fusion.46
  315.4 0.2 multiply_reduce_fusion
  315.7 0.8 add_convert_fusion
  (47 shorter events, 1.5 us)
Async XLA Ops:
  6.5 289.7 %copy-start = (bf16[512,1024]{1,0:T(8,128)(2,1)S(1)}, bf16[512,1024]{1,0:T(8,128)(2,1)}, u32[]{:S(2)}) copy-start(bf16[512,1024]{1,0:T(8,128)(2,1)} %param.19) | copy-start | bytes 3145732
  12.5 105.4 %all-to-all-start.1 = ((bf16[32,512,128]{2,1,0:T(8,128)(2,1)}), bf16[32,512,128]{2,1,0:T(8,128)(2,1)}, u32[]{:S(2)}, u32[]{:S(2)}) async-start(bf16[32,512,128]{2,1,0:T(8,128)(2,1)} %get-tuple-element.13), calls=%async_computation.1 | async-start | bytes 8388608 | tf_op jit(solution)/shard_map/all_to_all | solution.py:147
  118.0 8.5 %copy-start.11 = (s32[32]{0:T(128)S(1)}, s32[32]{0:T(128)}, u32[]{:S(2)}) copy-start(s32[32]{0:T(128)} %param.27) | copy-start | bytes 388
  118.0 9.1 %copy-start.12 = (s32[32]{0:T(128)S(1)}, s32[32]{0:T(128)}, u32[]{:S(2)}) copy-start(s32[32]{0:T(128)} %param.26) | copy-start | bytes 388
  118.0 9.7 %copy-start.2 = (bf16[1024,3,128]{2,0,1:T(8,128)(2,1)S(1)}, bf16[1024,3,128]{2,0,1:T(8,128)(2,1)}, u32[]{:S(2)}) copy-start(bf16[1024,3,128]{2,0,1:T(8,128)(2,1)} %param.15) | copy-start | bytes 2359300
  118.0 101.3 %all-to-all-start = ((bf16[32,128,512]{2,1,0:T(8,128)(2,1)}), bf16[32,128,512]{2,1,0:T(8,128)(2,1)}, u32[]{:S(2)}, u32[]{:S(2)}) async-start(bf16[32,128,512]{2,1,0:T(8,128)(2,1)} %bitcast.58), calls=%async_computation | async-start | bytes 8388608 | tf_op jit(solution)/shard_map/all_to_all | solution.py:146
  125.0 58.5 %all-gather.3.cloned.1.call-start = ((), (), s32[]{:S(2)}) async-start(), calls=%async_computation.5 | async-start | bytes 1179648 | tf_op jit(solution)/shard_map/all_gather | solution.py:149
  125.7 147.6 %all-gather.5.cloned.1.call-start = ((), (), s32[]{:S(2)}) async-start(), calls=%async_computation.6 | async-start | bytes 2359296 | tf_op jit(solution)/shard_map/all_gather | solution.py:158
  264.4 1.5 copy-start.4
  264.4 1.8 copy-start.1
  265.8 13.9 %copy-start.3 = (bf16[64,1024]{1,0:T(8,128)(2,1)S(1)}, bf16[64,1024]{1,0:T(8,128)(2,1)}, u32[]{:S(2)}) copy-start(bf16[64,1024]{1,0:T(8,128)(2,1)} %param.14) | copy-start | bytes 393220
  266.6 15.5 %copy-start.5 = (f32[1024]{0:T(1024)S(1)}, f32[1024]{0:T(1024)}, u32[]{:S(2)}) copy-start(f32[1024]{0:T(1024)} %param.22) | copy-start | bytes 12292
  266.6 15.5 %copy-start.6 = (f32[1024]{0:T(1024)S(1)}, f32[1024]{0:T(1024)}, u32[]{:S(2)}) copy-start(f32[1024]{0:T(1024)} %param.21) | copy-start | bytes 12292
  267.7 12.0 %all-to-all-start.2 = ((bf16[8,64,128]{2,1,0:T(8,128)(2,1)}), bf16[8,64,128]{2,1,0:T(8,128)(2,1)S(1)}, u32[]{:S(2)}, u32[]{:S(2)}) async-start(bf16[8,64,128]{2,1,0:T(8,128)(2,1)} %copy.30), calls=%async_computation.2 | async-start | bytes 262144 | tf_op jit(solution)/shard_map/all_to_all | solution.py:174
  281.8 14.3 %copy-start.10 = (f32[512]{0:T(512)S(1)}, f32[512]{0:T(512)}, u32[]{:S(2)}) copy-start(f32[512]{0:T(512)} %param.18) | copy-start | bytes 6148
  300.8 14.4 %copy-start.7 = (f32[1024]{0:T(1024)S(1)}, f32[1024]{0:T(1024)}, u32[]{:S(2)}) copy-start(f32[1024]{0:T(1024)} %param.20) | copy-start | bytes 12292
  300.8 14.8 %copy-start.8 = (f32[1024]{0:T(1024)S(1)}, f32[1024]{0:T(1024)}, u32[]{:S(2)}) copy-start(f32[1024]{0:T(1024)} %param.24) | copy-start | bytes 12292
  300.8 14.8 %copy-start.9 = (f32[1024]{0:T(1024)S(1)}, f32[1024]{0:T(1024)}, u32[]{:S(2)}) copy-start(f32[1024]{0:T(1024)} %param.23) | copy-start | bytes 12292
Sparse Core Ops, SparseCore 0:
  127.6 55.8 all-gather.2
  185.3 63.9 all-gather.4

commit v5 on v4

--- a/solution.py
+++ b/solution.py
@@ -1,3 +1,5 @@
+import functools
+
 import jax
 import jax.numpy as jnp
 from jax import lax
@@ -6,6 +8,7 @@
 from jax.sharding import PartitionSpec as P
 
 HEAD_DIM = 64
+CHUNKS = 2
 
 masked_score = -1e30
 
@@ -38,11 +41,11 @@
     return (jnp.squeeze(highest, axis=axis), sums_out, blend_out)
 
 
-def cache_kernel(count_ref, q_ref, kt_ref, v_ref, acc_ref, peak_ref):
+def cache_kernel(stride, offset, count_ref, q_ref, kt_ref, v_ref, acc_ref, peak_ref):
     block = pl.program_id(0)
     heads = q_ref.shape[0]
     width = kt_ref.shape[2]
-    start = block * width
+    start = block * stride + offset
     scale = HEAD_DIM ** (-0.5)
 
     @pl.when(block == 0)
@@ -85,7 +88,7 @@
         step(True)
 
 
-def cache_partials(queries, own_key_cols, own_values, cached_count):
+def cache_partials(queries, own_key_cols, own_values, cached_count, stride, offset):
     span, width = queries.shape
     total_blocks, block_width = own_values.shape[0], own_values.shape[1]
     heads = width // HEAD_DIM
@@ -104,7 +107,7 @@
         ],
     )
     acc, peaks = pl.pallas_call(
-        cache_kernel,
+        functools.partial(cache_kernel, stride, offset),
         grid_spec=grid_spec,
         out_shape=[
             jax.ShapeDtypeStruct((heads, span, width), jnp.float32),
@@ -143,8 +146,16 @@
     heads_here = width_here // HEAD_DIM
     where_req = lax.axis_index("req")
 
-    own_key_cols = lax.all_to_all(jnp.swapaxes(kv_cache[0], 1, 2), "req", split_axis=0, concat_axis=0, tiled=True)
-    own_values = lax.all_to_all(kv_cache[1], "req", split_axis=0, concat_axis=0, tiled=True)
+    block_len = kv_cache.shape[2]
+    chunk_len = block_len // CHUNKS
+    moved = []
+    for chunk in range(CHUNKS):
+        rows = slice(chunk * chunk_len, (chunk + 1) * chunk_len)
+        own_values = lax.all_to_all(kv_cache[1][:, rows], "req", split_axis=0, concat_axis=0, tiled=True)
+        own_key_cols = lax.all_to_all(
+            jnp.swapaxes(kv_cache[0][:, rows], 1, 2), "req", split_axis=0, concat_axis=0, tiled=True
+        )
+        moved.append((own_key_cols, own_values))
 
     span_rows = lax.all_gather(tokens, "tp", axis=0, tiled=True)
     flat_qkv = w_qkv.reshape(w_qkv.shape[0], 3 * width_here)
@@ -163,22 +174,26 @@
     allowed = (positions[None, :] <= positions[:, None]) & (positions[None, :] < fresh_count)
     fresh = partial_attention(queries, fresh_keys, fresh_values, allowed)
 
-    peaks, weight_sums, blended = cache_partials(heads_qkv[:, :width_here], own_key_cols, own_values, cached_count)
+    terms = [fresh] + [
+        cache_partials(heads_qkv[:, :width_here], key_cols, values, cached_count, block_len, chunk * chunk_len)
+        for chunk, (key_cols, values) in enumerate(moved)
+    ]
     peaks, weight_sums, blended = merge_axis(
-        jnp.stack([fresh[0], peaks]),
-        jnp.stack([fresh[1], weight_sums]),
-        jnp.stack([fresh[2], blended]),
+        jnp.stack([term[0] for term in terms]),
+        jnp.stack([term[1] for term in terms]),
+        jnp.stack([term[2] for term in terms]),
         0,
     )
     attention = (blended / jnp.repeat(weight_sums, HEAD_DIM, axis=-1)).astype(jnp.bfloat16)
-    attention = lax.all_to_all(attention, "tp", split_axis=0, concat_axis=1, tiled=True)
+    n_tp = lax.axis_size("tp")
+    attention = lax.all_to_all(
+        jnp.broadcast_to(attention[None], (n_tp,) + attention.shape), "tp", split_axis=0, concat_axis=2, tiled=True
+    ).reshape(span, -1)
 
     projected = jnp.dot(attention, full_out, preferred_element_type=jnp.float32)
-    normed = layer_norm(tokens.astype(jnp.float32) + projected, ln1_gain, ln1_bias).astype(jnp.bfloat16)
-    n_tp = lax.axis_size("tp")
-    span_normed = lax.all_to_all(
-        jnp.broadcast_to(normed[None], (n_tp,) + normed.shape), "tp", split_axis=0, concat_axis=0, tiled=True
-    ).reshape(-1, normed.shape[1])
+    span_normed = layer_norm(span_rows.astype(jnp.float32) + projected, ln1_gain, ln1_bias).astype(jnp.bfloat16)
+    rows_here = tokens.shape[0]
+    normed = lax.dynamic_slice_in_dim(span_normed, lax.axis_index("tp") * rows_here, rows_here)
     hidden = jax.nn.gelu(
         jnp.dot(span_normed, w_up, preferred_element_type=jnp.float32) + b_up,
         approximate=False,

time: 324 us -> 411 us (1.27)
  the two profiles are of different devices: /device:TPU:80 before, /device:TPU:193 now
where the time goes in v5:
time: 411 us; the launch traced here: 407 us
  waiting for transfers between devices  117 us (28%)
  blocking collectives  113 us (27%)
  Pallas kernels  85.7 us (21%)
  local copies, waits for them, and re-layouts  32 us (8%)
  starting transfers between devices  26 us (6%)
  between operations  13.7 us (3%)
  matrix products  12.4 us (3%)
  other arithmetic  6.42 us (2%)
    pallas_call x2, Pallas kernels, cache_partials(): pl.pallas_call(functools.partial(cache_kernel, stride, offset), grid_spec...  85.7 us
    all_to_all x1, blocking collectives, shards(): lax.all_to_all(kv_cache[1][:, rows], 'req', split_axis=0, concat_axis=0,...  56.8 us
    all_to_all x1, blocking collectives, shards(): lax.all_to_all(jnp.swapaxes(kv_cache[0][:, rows], 1, 2), 'req', split_axi...  56.3 us
    all_gather x1, waiting for transfers between devices, shards(): span_rows = lax.all_gather(tokens, 'tp', axis=0, tiled=True)  46.9 us
    all_to_all x1, waiting for transfers between devices, shards(): lax.all_to_all(jnp.swapaxes(kv_cache[0][:, rows], 1, 2), 'req', split_axi...  43.2 us
    all_to_all x1, waiting for transfers between devices, shards(): lax.all_to_all(jnp.broadcast_to(attention[None], (n_tp,) + attention.shap...  15.8 us
    unnamed x34, local copies, waits for them, and re-layouts  11.3 us
    all_to_all x1, waiting for transfers between devices, shards(): lax.all_to_all(partial.reshape((n_tp, -1) + partial.shape[1:]), 'tp', spl...  10.1 us
  transfers between devices with their start and end apart: 6, of which 4 were waited for; matrix products, arithmetic and copies ran while one was open for 6% of the time, Pallas kernels for 21%

profile of v5, /device:TPU:193, one launch (start us, length us, event | category | flops | bytes accessed | tf_op | source)
XLA Modules:
  0.0 406.5 jit_solution(6118180648923616040)
XLA Ops:
  6.5 6.0 %slice_bitcast_fusion = (bf16[32,512,128]{2,1,0:T(8,128)(2,1)}, bf16[1,32,512,128]{3,2,1,0:T(8,128)(2,1)}) fusion(bf16[2,32,512,128]{3,2,1,0:T(8,128)(2,1)} %param.25), kind=kLoop, calls=%fused_computation | loop fusion | bytes 16777216 | tf_op jit(solution)/shard_map/squeeze | solution.py:154
  12.5 6.5 %copy.27 = bf16[1,32,512,128]{2,3,1,0:T(8,128)(2,1)} copy(bf16[1,32,512,128]{3,2,1,0:T(8,128)(2,1)} %get-tuple-element.20) | data formatting | bytes 8388608
  19.1 4.0 slice_bitcast_fusion.2
  23.0 9.5 %all-to-all-start = ((bf16[32,128,256]{2,1,0:T(8,128)(2,1)}), bf16[32,128,256]{2,1,0:T(8,128)(2,1)}, u32[]{:S(2)}, u32[]{:S(2)}) async-start(bf16[32,128,256]{2,1,0:T(8,128)(2,1)} %get-tuple-element.23), calls=%async_computation | async-start | bytes 4194304 | tf_op jit(solution)/shard_map/all_to_all | solution.py:155
  32.5 4.7 %fusion.78 = (bf16[32,256,128]{2,1,0:T(8,128)(2,1)}, bf16[32,256,128]{2,1,0:T(8,128)(2,1)}) fusion(bf16[32,512,128]{2,1,0:T(8,128)(2,1)} %get-tuple-element.19), kind=kLoop, calls=%fused_computation.127 | loop fusion | bytes 8388608 | tf_op jit(solution)/shard_map/slice | solution.py:154
  37.3 43.2 %all-to-all-done.kt_ref = bf16[32,128,256]{2,1,0:T(8,128)(2,1)} async-done(((bf16[32,128,256]{2,1,0:T(8,128)(2,1)}), bf16[32,128,256]{2,1,0:T(8,128)(2,1)}, u32[]{:S(2)}, u32[]{:S(2)}) %all-to-all-start) | async-done | bytes 2097184 | tf_op jit(solution)/shard_map/all_to_all | solution.py:155
  80.5 56.8 %all_to_all.40.v_ref = bf16[32,256,128]{2,1,0:T(8,128)(2,1)} all-to-all(bf16[32,256,128]{2,1,0:T(8,128)(2,1)} %get-tuple-element.21), channel_id=1, replica_groups=mesh['req'=32,'tp'=8] {'req'}, dimensions={0} | all-to-all | bytes 4194304 | tf_op jit(solution)/shard_map/all_to_all | solution.py:154
  137.3 56.3 %all_to_all.41.kt_ref = bf16[32,128,256]{2,1,0:T(8,128)(2,1)} all-to-all(bf16[32,128,256]{2,1,0:T(8,128)(2,1)S(1)} %get-tuple-element.24), channel_id=1, replica_groups=mesh['req'=32,'tp'=8] {'req'}, dimensions={0} | all-to-all | bytes 4194304 | tf_op jit(solution)/shard_map/all_to_all | solution.py:155
  193.6 8.4 %all-to-all-start.3 = ((bf16[32,256,128]{2,1,0:T(8,128)(2,1)}), bf16[32,256,128]{2,1,0:T(8,128)(2,1)S(1)}, u32[]{:S(2)}, u32[]{:S(2)}) async-start(bf16[32,256,128]{2,1,0:T(8,128)(2,1)} %get-tuple-element.22), calls=%async_computation.3 | async-start | bytes 4194304 | tf_op jit(solution)/shard_map/all_to_all | solution.py:154
  202.0 0.7 all-gather.3.cloned.1.call-update
  203.4 2.3 copy.20
  206.9 0.6 iota_compare_fusion.1
  207.7 46.9 %all-gather.3.cloned.1.call-done = bf16[512,1024]{1,0:T(8,128)(2,1)} async-done(((bf16[64,1024]{1,0:T(8,128)(2,1)}), bf16[512,1024]{1,0:T(8,128)(2,1)}) %all-gather.3.cloned.1.call-update) | async-done | bytes 1048592 | tf_op jit(solution)/shard_map/all_gather | solution.py:160
  254.6 2.1 convolution_convert_fusion.1
  256.7 0.7 fusion.79
  257.4 0.8 copy.21
  258.2 1.6 fusion
  260.4 1.5 convolution_bitcast_fusion
  261.8 42.8 %shard_map.136 = (f32[2,512,128]{2,1,0:T(8,128)}, f32[2,512,1]{2,1,0:T(8,128)}) custom-call(s32[1]{0:T(128)} %dynamic_slice.10.count_ref, bf16[2,512,64]{2,1,0:T(8,128)(2,1)} %bitcast.78, bf16[32,128,256]{2,1,0:T(8,128)(2,1)} %all-to-all-done.kt_ref, bf16[32,256,128]{2,1,0:T(8,128)(2,1)} %all_to_all.40.v_ref), custom_call_target="tpu_custom_call" | custom-call | flops 3221225472 | bytes 4849664 | tf_op jit(solution)/shard_map/pallas_call | solution.py:109
  304.7 1.3 reduce.4
  306.0 1.3 copy-done.1
  307.3 42.9 %shard_map.137 = (f32[2,512,128]{2,1,0:T(8,128)}, f32[2,512,1]{2,1,0:T(8,128)}) custom-call(s32[1]{0:T(128)} %dynamic_slice.10.count_ref, bf16[2,512,64]{2,1,0:T(8,128)(2,1)} %bitcast.79, bf16[32,128,256]{2,1,0:T(8,128)(2,1)} %all_to_all.41.kt_ref, bf16[32,256,128]{2,1,0:T(8,128)(2,1)} %copy-done.1), custom_call_target="tpu_custom_call" | custom-call | flops 3221225472 | bytes 4849664 | tf_op jit(solution)/shard_map/pallas_call | solution.py:109
  350.1 1.3 reduce.5
  351.4 1.2 slice_bitcast_fusion.6
  354.5 1.1 broadcast_in_dim.29
  355.6 4.2 %all-to-all-start.4 = ((bf16[8,512,128]{1,2,0:T(8,128)(2,1)}), bf16[8,512,128]{1,2,0:T(8,128)(2,1)S(1)}, u32[]{:S(2)}, u32[]{:S(2)}) async-start(bf16[8,512,128]{1,2,0:T(8,128)(2,1)} %broadcast_in_dim.29), calls=%async_computation.4 | async-start | bytes 2097152 | tf_op jit(solution)/shard_map/all_to_all | solution.py:189
  359.8 15.8 %all-to-all-done.4 = bf16[8,512,128]{1,2,0:T(8,128)(2,1)S(1)} async-done(((bf16[8,512,128]{1,2,0:T(8,128)(2,1)}), bf16[8,512,128]{1,2,0:T(8,128)(2,1)S(1)}, u32[]{:S(2)}, u32[]{:S(2)}) %all-to-all-start.4) | async-done | bytes 1048608 | tf_op jit(solution)/shard_map/all_to_all | solution.py:189
  375.6 2.9 fusion.80
  380.1 4.4 %convolution_convert_fusion = bf16[512,1024]{1,0:T(8,128)(2,1)} fusion(bf16[512,1024]{1,0:T(8,128)(2,1)S(1)} %copy-done, bf16[512,1024]{1,0:T(8,128)(2,1)S(1)} %add_convert_fusion, bf16[1024,512]{1,0:T(8,128)(2,1)S(1)} %copy-done.12, f32[512]{0:T(512)S(1)} %copy-done.13), kind=kOutput, calls=%fused_computation.12 | convolution fusion | flops 1091567616 | bytes 4196352 | tf_op jit(solution)/shard_map/dot_general | solution.py:201
  384.5 3.7 all-to-all-start.5
  388.2 10.1 %all-to-all-done.5 = bf16[8,64,1024]{2,1,0:T(8,128)(2,1)S(1)} async-done(((bf16[8,64,1024]{2,1,0:T(8,128)(2,1)}), bf16[8,64,1024]{2,1,0:T(8,128)(2,1)S(1)}, u32[]{:S(2)}, u32[]{:S(2)}) %all-to-all-start.5) | async-done | bytes 1048608 | tf_op jit(solution)/shard_map/all_to_all | solution.py:202
  398.9 0.8 add_convert_fusion.1
  (61 shorter events, 6.6 us)
Async XLA Ops:
  6.5 373.1 %copy-start = (bf16[512,1024]{1,0:T(8,128)(2,1)S(1)}, bf16[512,1024]{1,0:T(8,128)(2,1)}, u32[]{:S(2)}) copy-start(bf16[512,1024]{1,0:T(8,128)(2,1)} %param.19) | copy-start | bytes 3145732
  23.0 57.5 %all-to-all-start = ((bf16[32,128,256]{2,1,0:T(8,128)(2,1)}), bf16[32,128,256]{2,1,0:T(8,128)(2,1)}, u32[]{:S(2)}, u32[]{:S(2)}) async-start(bf16[32,128,256]{2,1,0:T(8,128)(2,1)} %get-tuple-element.23), calls=%async_computation | async-start | bytes 4194304 | tf_op jit(solution)/shard_map/all_to_all | solution.py:155
  193.6 12.2 %copy-start.14 = (s32[32]{0:T(128)S(1)}, s32[32]{0:T(128)}, u32[]{:S(2)}) copy-start(s32[32]{0:T(128)} %param.26) | copy-start | bytes 388
  193.6 12.8 %copy-start.15 = (s32[32]{0:T(128)S(1)}, s32[32]{0:T(128)}, u32[]{:S(2)}) copy-start(s32[32]{0:T(128)} %param.27) | copy-start | bytes 388
  193.6 112.4 %all-to-all-start.3 = ((bf16[32,256,128]{2,1,0:T(8,128)(2,1)}), bf16[32,256,128]{2,1,0:T(8,128)(2,1)S(1)}, u32[]{:S(2)}, u32[]{:S(2)}) async-start(bf16[32,256,128]{2,1,0:T(8,128)(2,1)} %get-tuple-element.22), calls=%async_computation.3 | async-start | bytes 4194304 | tf_op jit(solution)/shard_map/all_to_all | solution.py:154
  201.9 52.7 %all-gather.3.cloned.1.call-start = ((), (), s32[]{:S(2)}) async-start(), calls=%async_computation.6 | async-start | bytes 1179648 | tf_op jit(solution)/shard_map/all_gather | solution.py:160
  202.7 157.1 %all-gather.5.cloned.1.call-start = ((), (), s32[]{:S(2)}) async-start(), calls=%async_computation.7 | async-start | bytes 2359296 | tf_op jit(solution)/shard_map/all_gather | solution.py:169
  258.2 2.1 copy-start.6
  306.0 1.3 copy-start.1
  350.1 2.8 copy-start.3
  352.6 1.0 copy-start.2
  352.8 1.6 copy-start.5
  354.4 21.1 %copy-start.4 = (bf16[512,1024]{1,0:T(8,128)(2,1)S(1)}, bf16[512,1024]{1,0:T(8,128)(2,1)}, u32[]{:S(2)}) copy-start(bf16[512,1024]{1,0:T(8,128)(2,1)} %all-gather.3.cloned.1.call-done) | copy-start | bytes 3145732
  355.6 20.0 %all-to-all-start.4 = ((bf16[8,512,128]{1,2,0:T(8,128)(2,1)}), bf16[8,512,128]{1,2,0:T(8,128)(2,1)S(1)}, u32[]{:S(2)}, u32[]{:S(2)}) async-start(bf16[8,512,128]{1,2,0:T(8,128)(2,1)} %broadcast_in_dim.29), calls=%async_computation.4 | async-start | bytes 2097152 | tf_op jit(solution)/shard_map/all_to_all | solution.py:189
  378.5 0.7 copy-start.8
  378.5 0.7 copy-start.9
  378.9 1.2 copy-start.12
  378.9 1.2 copy-start.13
  384.5 14.0 %copy-start.7 = (f32[1024]{0:T(1024)S(1)}, f32[1024]{0:T(1024)}, u32[]{:S(2)}) copy-start(f32[1024]{0:T(1024)} %param.20) | copy-start | bytes 12292
  384.5 14.4 %copy-start.10 = (f32[1024]{0:T(1024)S(1)}, f32[1024]{0:T(1024)}, u32[]{:S(2)}) copy-start(f32[1024]{0:T(1024)} %param.24) | copy-start | bytes 12292
  384.5 14.4 %copy-start.11 = (f32[1024]{0:T(1024)S(1)}, f32[1024]{0:T(1024)}, u32[]{:S(2)}) copy-start(f32[1024]{0:T(1024)} %param.23) | copy-start | bytes 12292
  384.5 13.8 %all-to-all-start.5 = ((bf16[8,64,1024]{2,1,0:T(8,128)(2,1)}), bf16[8,64,1024]{2,1,0:T(8,128)(2,1)S(1)}, u32[]{:S(2)}, u32[]{:S(2)}) async-start(bf16[8,64,1024]{2,1,0:T(8,128)(2,1)} %bitcast.71), calls=%async_computation.5 | async-start | bytes 2097152 | tf_op jit(solution)/shard_map/all_to_all | solution.py:202
Sparse Core Ops, SparseCore 0:
  204.6 49.9 all-gather.2
  256.4 55.3 all-gather.4

commit v6 on v4

--- a/solution.py
+++ b/solution.py
@@ -38,21 +38,15 @@
     return (jnp.squeeze(highest, axis=axis), sums_out, blend_out)
 
 
-def cache_kernel(count_ref, q_ref, kt_ref, v_ref, acc_ref, peak_ref):
+def score_kernel(count_ref, q_ref, kt_ref, w_ref, peak_ref):
     block = pl.program_id(0)
     heads = q_ref.shape[0]
     width = kt_ref.shape[2]
     start = block * width
     scale = HEAD_DIM ** (-0.5)
 
-    @pl.when(block == 0)
-    def _():
-        acc_ref[...] = jnp.zeros_like(acc_ref)
-        peak_ref[...] = jnp.full_like(peak_ref, masked_score)
-
     def step(masked):
         allowed = start + lax.broadcasted_iota(jnp.int32, (1, width), 1) < count_ref[0]
-        lane = lax.broadcasted_iota(jnp.int32, (1, v_ref.shape[2]), 1)
         for head in range(heads):
             raw = jnp.dot(
                 q_ref[head], kt_ref[0, head * HEAD_DIM : (head + 1) * HEAD_DIM, :], preferred_element_type=jnp.float32
@@ -63,31 +57,54 @@
             weights = jnp.exp((raw - top) * scale)
             if masked:
                 weights = jnp.where(allowed, weights, 0.0)
-            weights = weights.astype(jnp.bfloat16)
+            w_ref[0, head] = weights.astype(jnp.bfloat16)
+            peak_ref[0, head] = top * scale
+
+    full = start + width <= count_ref[0]
+    some = start < count_ref[0]
+
+    @pl.when(full)
+    def _():
+        step(False)
+
+    @pl.when(some & jnp.logical_not(full))
+    def _():
+        step(True)
+
+    @pl.when(jnp.logical_not(some))
+    def _():
+        w_ref[...] = jnp.zeros_like(w_ref)
+        peak_ref[...] = jnp.full_like(peak_ref, masked_score)
+
+
+def blend_kernel(count_ref, w_ref, block_peak_ref, v_ref, acc_ref, peak_ref):
+    block = pl.program_id(0)
+    heads = w_ref.shape[1]
+    width = v_ref.shape[1]
+    start = block * width
+
+    @pl.when(block == 0)
+    def _():
+        acc_ref[...] = jnp.zeros_like(acc_ref)
+        peak_ref[...] = jnp.full_like(peak_ref, masked_score)
+
+    @pl.when(start < count_ref[0])
+    def _():
+        lane = lax.broadcasted_iota(jnp.int32, (1, v_ref.shape[2]), 1)
+        for head in range(heads):
             own = (lane >= head * HEAD_DIM) & (lane < (head + 1) * HEAD_DIM)
             values = jnp.where(own, v_ref[0], jnp.ones_like(v_ref[0]))
-            blend = jnp.dot(weights, values, preferred_element_type=jnp.float32)
-            peak = top * scale
+            blend = jnp.dot(w_ref[0, head], values, preferred_element_type=jnp.float32)
+            peak = block_peak_ref[0, head]
             old = peak_ref[head]
             new = jnp.maximum(old, peak)
             peak_ref[head] = new
             acc_ref[head] = acc_ref[head] * jnp.exp(old - new) + blend * jnp.exp(peak - new)
 
-    full = start + width <= count_ref[0]
-    some = start < count_ref[0]
-
-    @pl.when(full)
-    def _():
-        step(False)
-
-    @pl.when(some & jnp.logical_not(full))
-    def _():
-        step(True)
-
-
-def cache_partials(queries, own_key_cols, own_values, cached_count):
+
+def block_weights(queries, own_key_cols, cached_count):
     span, width = queries.shape
-    total_blocks, block_width = own_values.shape[0], own_values.shape[1]
+    total_blocks, block_width = own_key_cols.shape[0], own_key_cols.shape[2]
     heads = width // HEAD_DIM
     per_head = queries.reshape(span, heads, HEAD_DIM).transpose(1, 0, 2)
     grid_spec = pltpu.PrefetchScalarGridSpec(
@@ -96,6 +113,37 @@
         in_specs=[
             pl.BlockSpec((heads, span, HEAD_DIM), lambda b, c: (0, 0, 0)),
             pl.BlockSpec((1, width, block_width), lambda b, c: (b, 0, 0)),
+        ],
+        out_specs=[
+            pl.BlockSpec((1, heads, span, block_width), lambda b, c: (b, 0, 0, 0)),
+            pl.BlockSpec((1, heads, span, 1), lambda b, c: (b, 0, 0, 0)),
+        ],
+    )
+    return pl.pallas_call(
+        score_kernel,
+        grid_spec=grid_spec,
+        out_shape=[
+            jax.ShapeDtypeStruct((total_blocks, heads, span, block_width), jnp.bfloat16),
+            jax.ShapeDtypeStruct((total_blocks, heads, span, 1), jnp.float32),
+        ],
+        compiler_params=pltpu.CompilerParams(dimension_semantics=("arbitrary",)),
+        cost_estimate=pl.CostEstimate(
+            flops=2 * span * block_width * HEAD_DIM * heads * total_blocks,
+            transcendentals=heads * span * block_width * total_blocks,
+            bytes_accessed=own_key_cols.size * 2 + total_blocks * heads * span * block_width * 2,
+        ),
+    )(jnp.reshape(cached_count, (1,)), per_head, own_key_cols)
+
+
+def cache_partials(weights, block_peaks, own_values, cached_count):
+    total_blocks, heads, span, block_width = weights.shape
+    width = own_values.shape[2]
+    grid_spec = pltpu.PrefetchScalarGridSpec(
+        num_scalar_prefetch=1,
+        grid=(total_blocks,),
+        in_specs=[
+            pl.BlockSpec((1, heads, span, block_width), lambda b, c: (b, 0, 0, 0)),
+            pl.BlockSpec((1, heads, span, 1), lambda b, c: (b, 0, 0, 0)),
             pl.BlockSpec((1, block_width, width), lambda b, c: (b, 0, 0)),
         ],
         out_specs=[
@@ -104,7 +152,7 @@
         ],
     )
     acc, peaks = pl.pallas_call(
-        cache_kernel,
+        blend_kernel,
         grid_spec=grid_spec,
         out_shape=[
             jax.ShapeDtypeStruct((heads, span, width), jnp.float32),
@@ -112,11 +160,11 @@
         ],
         compiler_params=pltpu.CompilerParams(dimension_semantics=("arbitrary",)),
         cost_estimate=pl.CostEstimate(
-            flops=2 * span * block_width * (HEAD_DIM + width) * heads * total_blocks,
-            transcendentals=heads * span * block_width * total_blocks,
-            bytes_accessed=own_values.size * 4 + span * width * 2 + heads * span * width * 4,
+            flops=2 * span * block_width * width * heads * total_blocks,
+            transcendentals=2 * heads * span * total_blocks,
+            bytes_accessed=weights.size * 2 + own_values.size * 2 + heads * span * width * 4,
         ),
-    )(jnp.reshape(cached_count, (1,)), per_head, own_key_cols, own_values)
+    )(jnp.reshape(cached_count, (1,)), weights, block_peaks, own_values)
     spare = [((head + 1) % heads) * HEAD_DIM for head in range(heads)]
     blended = jnp.concatenate([acc[head, :, head * HEAD_DIM : (head + 1) * HEAD_DIM] for head in range(heads)], axis=1)
     sums = jnp.stack([acc[head, :, spare[head]] for head in range(heads)], axis=1)
@@ -144,7 +192,8 @@
     where_req = lax.axis_index("req")
 
     own_key_cols = lax.all_to_all(jnp.swapaxes(kv_cache[0], 1, 2), "req", split_axis=0, concat_axis=0, tiled=True)
-    own_values = lax.all_to_all(kv_cache[1], "req", split_axis=0, concat_axis=0, tiled=True)
+    own_key_cols, values_here = lax.optimization_barrier((own_key_cols, kv_cache[1]))
+    own_values = lax.all_to_all(values_here, "req", split_axis=0, concat_axis=0, tiled=True)
 
     span_rows = lax.all_gather(tokens, "tp", axis=0, tiled=True)
     flat_qkv = w_qkv.reshape(w_qkv.shape[0], 3 * width_here)
@@ -163,7 +212,8 @@
     allowed = (positions[None, :] <= positions[:, None]) & (positions[None, :] < fresh_count)
     fresh = partial_attention(queries, fresh_keys, fresh_values, allowed)
 
-    peaks, weight_sums, blended = cache_partials(heads_qkv[:, :width_here], own_key_cols, own_values, cached_count)
+    weights, block_peaks = block_weights(heads_qkv[:, :width_here], own_key_cols, cached_count)
+    peaks, weight_sums, blended = cache_partials(weights, block_peaks, own_values, cached_count)
     peaks, weight_sums, blended = merge_axis(
         jnp.stack([fresh[0], peaks]),
         jnp.stack([fresh[1], weight_sums]),

time: 324 us -> 327 us (level); the launches traced: 323 us -> 321 us
  waiting for transfers between devices: 182 us -> 66.3 us
  blocking collectives: 28 us -> 142 us
  starting transfers between devices: 23.4 us -> 13.2 us
  Pallas kernels: 45.2 us -> 54.7 us
    all_to_all x2 -> x1, waiting for transfers between devices: 119 us -> 3.73 us  [shards(): lax.all_to_all(values_here, 'req', split_axis=0, concat_axis=0, tiled=True)]
    all_to_all x0 -> x1, blocking collectives: none -> 105 us  [shards(): lax.all_to_all(jnp.swapaxes(kv_cache[0], 1, 2), 'req', split_axis=0, conc...]
    all_to_all x2 -> x1, starting transfers between devices: 17.7 us -> 7.6 us  [shards(): lax.all_to_all(values_here, 'req', split_axis=0, concat_axis=0, tiled=True)]
    pallas_call x1 -> x2, Pallas kernels: 45.2 us -> 54.7 us  [the longest x1 27.3 us: cache_partials(): pl.pallas_call(blend_kernel, grid_spec=grid_spec, out_shape=[jax.ShapeDty...]
    all_to_all x1, blocking collectives: 13.9 us -> 18.8 us  [shards(): lax.all_to_all(jnp.broadcast_to(normed[None], (n_tp,) + normed.shape), 't...]
    all_to_all x1, blocking collectives: 14.2 us -> 18.6 us  [shards(): lax.all_to_all(partial.reshape((n_tp, -1) + partial.shape[1:]), 'tp', spl...]
  transfers between devices with their start and end apart: 5 -> 4, of which waited for: 4 -> 3; matrix products, arithmetic and copies ran while one was open for 5% -> 3% of each run, Pallas kernels for 14% -> 17%
where the time goes in v6:
time: 327 us; the launch traced here: 321 us
  blocking collectives  142 us (43%)
  waiting for transfers between devices  66.3 us (20%)
  Pallas kernels  54.7 us (17%)
  local copies, waits for them, and re-layouts  17.8 us (5%)
  between operations  13.7 us (4%)
  starting transfers between devices  13.2 us (4%)
  matrix products  10 us (3%)
  other arithmetic  3.66 us (1%)
    all_to_all x1, blocking collectives, shards(): lax.all_to_all(jnp.swapaxes(kv_cache[0], 1, 2), 'req', split_axis=0, conc...  105 us
    all_gather x1, waiting for transfers between devices, shards(): span_rows = lax.all_gather(tokens, 'tp', axis=0, tiled=True)  54.6 us
    pallas_call x1, Pallas kernels, cache_partials(): pl.pallas_call(blend_kernel, grid_spec=grid_spec, out_shape=[jax.ShapeDty...  27.3 us
    pallas_call x1, Pallas kernels, block_weights(): pl.pallas_call(score_kernel, grid_spec=grid_spec, out_shape=[jax.ShapeDty...  27.3 us
    all_to_all x1, blocking collectives, shards(): lax.all_to_all(jnp.broadcast_to(normed[None], (n_tp,) + normed.shape), 't...  18.8 us
    all_to_all x1, blocking collectives, shards(): lax.all_to_all(partial.reshape((n_tp, -1) + partial.shape[1:]), 'tp', spl...  18.6 us
    all_to_all x1, starting transfers between devices, shards(): lax.all_to_all(values_here, 'req', split_axis=0, concat_axis=0, tiled=True)  7.6 us
    unnamed x28, local copies, waits for them, and re-layouts  6.81 us
  transfers between devices with their start and end apart: 4, of which 3 were waited for; matrix products, arithmetic and copies ran while one was open for 3% of the time, Pallas kernels for 17%

profile of v6, /device:TPU:80, one launch (start us, length us, event | category | flops | bytes accessed | tf_op | source)
XLA Modules:
  0.0 321.4 jit_solution(7395192585406681002)
XLA Ops:
  6.5 6.1 %slice_bitcast_fusion = (bf16[32,512,128]{2,1,0:T(8,128)(2,1)}, bf16[1,32,512,128]{3,2,1,0:T(8,128)(2,1)}) fusion(bf16[2,32,512,128]{3,2,1,0:T(8,128)(2,1)} %param.25), kind=kLoop, calls=%fused_computation | loop fusion | bytes 16777216 | tf_op jit(solution)/shard_map/squeeze | solution.py:195
  12.6 6.5 %copy.33 = bf16[1,32,512,128]{2,3,1,0:T(8,128)(2,1)} copy(bf16[1,32,512,128]{3,2,1,0:T(8,128)(2,1)} %get-tuple-element.22) | data formatting | bytes 8388608
  19.1 104.7 %all_to_all.36.kt_ref = bf16[32,128,512]{2,1,0:T(8,128)(2,1)} all-to-all(bf16[32,128,512]{2,1,0:T(8,128)(2,1)} %bitcast.58), channel_id=1, replica_groups=mesh['req'=32,'tp'=8] {'req'}, dimensions={0} | all-to-all | bytes 8388608 | tf_op jit(solution)/shard_map/all_to_all | solution.py:194
  123.8 7.6 %all-to-all-start.1 = ((bf16[32,512,128]{2,1,0:T(8,128)(2,1)}), bf16[32,512,128]{2,1,0:T(8,128)(2,1)}, u32[]{:S(2)}, u32[]{:S(2)}) async-start(bf16[32,512,128]{2,1,0:T(8,128)(2,1)} %get-tuple-element.14), calls=%async_computation.1 | async-start | bytes 8388608 | tf_op jit(solution)/shard_map/all_to_all | solution.py:196
  131.4 0.7 all-gather.3.cloned.1.call-update
  132.2 0.7 all-gather.5.cloned.1.call-update
  132.9 0.3 copy.25
  133.2 0.6 dynamic_slice.7.count_ref
  133.8 0.7 dynamic_slice.6
  134.5 0.7 iota_compare_fusion.1
  135.3 54.6 %all-gather.3.cloned.1.call-done = bf16[512,1024]{1,0:T(8,128)(2,1)} async-done(((bf16[64,1024]{1,0:T(8,128)(2,1)}), bf16[512,1024]{1,0:T(8,128)(2,1)}) %all-gather.3.cloned.1.call-update) | async-done | bytes 1048592 | tf_op jit(solution)/shard_map/all_gather | solution.py:198
  189.9 1.8 convolution_convert_fusion.1
  191.8 0.8 copy.26
  192.6 0.6 fusion
  193.2 0.8 convolution_bitcast_fusion
  194.0 0.6 convert_reduce_fusion.1
  194.6 27.3 %shard_map.136 = (bf16[32,2,512,512]{3,2,1,0:T(8,128)(2,1)}, f32[32,2,512,1]{3,2,1,0:T(8,128)}) custom-call(s32[1]{0:T(128)} %dynamic_slice.7.count_ref, bf16[2,512,64]{2,1,0:T(8,128)(2,1)} %bitcast.65, bf16[32,128,512]{2,1,0:T(8,128)(2,1)} %all_to_all.36.kt_ref), custom_call_target="tpu_custom_call" | custom-call | flops 2147483648 | bytes 37748736 | tf_op jit(solution)/shard_map/pallas_call | solution.py:122
  221.9 3.7 %all-to-all-done.1.v_ref = bf16[32,512,128]{2,1,0:T(8,128)(2,1)} async-done(((bf16[32,512,128]{2,1,0:T(8,128)(2,1)}), bf16[32,512,128]{2,1,0:T(8,128)(2,1)}, u32[]{:S(2)}, u32[]{:S(2)}) %all-to-all-start.1) | async-done | bytes 4194336 | tf_op jit(solution)/shard_map/all_to_all | solution.py:196
  225.6 27.3 %shard_map.137 = (f32[2,512,128]{2,1,0:T(8,128)}, f32[2,512,1]{2,1,0:T(8,128)}) custom-call(s32[1]{0:T(128)} %dynamic_slice.7.count_ref, bf16[32,2,512,512]{3,2,1,0:T(8,128)(2,1)} %get-tuple-element.12.w_ref, f32[32,2,512,1]{3,2,1,0:T(8,128)} %get-tuple-element.13.block_peak_ref, bf16[32,512,128]{2,1,0:T(8,128)(2,1)} %all-to-all-done.1.v_ref), custom_call_target="tpu_custom_call" | custom-call | flops 4294967296 | bytes 38273024 | tf_op jit(solution)/shard_map/pallas_call | solution.py:154
  253.0 1.3 slice_bitcast_fusion.2
  254.5 0.2 reduce.3
  254.7 0.3 slice_reduce_fusion.1
  255.4 0.8 copy.30
  256.3 5.5 %all-to-all-start.2 = ((bf16[8,64,128]{2,1,0:T(8,128)(2,1)}), bf16[8,64,128]{2,1,0:T(8,128)(2,1)S(1)}, u32[]{:S(2)}, u32[]{:S(2)}) async-start(bf16[8,64,128]{2,1,0:T(8,128)(2,1)} %copy.30), calls=%async_computation.2 | async-start | bytes 262144 | tf_op jit(solution)/shard_map/all_to_all | solution.py:224
  261.8 6.5 %all-to-all-done.2 = bf16[8,64,128]{2,1,0:T(8,128)(2,1)S(1)} async-done(((bf16[8,64,128]{2,1,0:T(8,128)(2,1)}), bf16[8,64,128]{2,1,0:T(8,128)(2,1)S(1)}, u32[]{:S(2)}, u32[]{:S(2)}) %all-to-all-start.2) | async-done | bytes 131104 | tf_op jit(solution)/shard_map/all_to_all | solution.py:224
  268.4 2.2 fusion.81
  271.0 18.8 %all_to_all.37 = bf16[8,64,1024]{2,1,0:T(8,128)(2,1)S(1)} all-to-all(bf16[8,64,1024]{2,1,0:T(8,128)(2,1)S(1)} %broadcast_in_dim.29), channel_id=1, replica_groups=mesh['req'=32,'tp'=8] {'tp'}, dimensions={0} | all-to-all | bytes 2097152 | tf_op jit(solution)/shard_map/all_to_all | solution.py:229
  289.9 4.6 %convolution_convert_fusion = bf16[512,1024]{1,0:T(8,128)(2,1)S(1)} fusion(bf16[512,1024]{1,0:T(8,128)(2,1)S(1)} %copy-done, bf16[512,1024]{1,0:T(8,128)(2,1)S(1)} %bitcast.60, bf16[1024,512]{1,0:T(8,128)(2,1)} %param.17, f32[512]{0:T(512)S(1)} %copy-done.10), kind=kOutput, calls=%fused_computation.7 | convolution fusion | flops 1091567616 | bytes 4196352 | tf_op jit(solution)/shard_map/dot_general | solution.py:236
  294.5 18.6 %all_to_all.38 = bf16[8,64,1024]{2,1,0:T(8,128)(2,1)S(1)} all-to-all(bf16[8,64,1024]{2,1,0:T(8,128)(2,1)S(1)} %bitcast.61), channel_id=1, replica_groups=mesh['req'=32,'tp'=8] {'tp'}, dimensions={0} | all-to-all | bytes 2097152 | tf_op jit(solution)/shard_map/all_to_all | solution.py:237
  313.3 0.2 fusion.46
  313.5 0.2 multiply_reduce_fusion
  313.8 0.8 add_convert_fusion
  (47 shorter events, 1.5 us)
Async XLA Ops:
  6.5 283.3 %copy-start = (bf16[512,1024]{1,0:T(8,128)(2,1)S(1)}, bf16[512,1024]{1,0:T(8,128)(2,1)}, u32[]{:S(2)}) copy-start(bf16[512,1024]{1,0:T(8,128)(2,1)} %param.19) | copy-start | bytes 3145732
  123.8 9.1 %copy-start.2 = (bf16[1024,3,128]{2,0,1:T(8,128)(2,1)S(1)}, bf16[1024,3,128]{2,0,1:T(8,128)(2,1)}, u32[]{:S(2)}) copy-start(bf16[1024,3,128]{2,0,1:T(8,128)(2,1)} %param.15) | copy-start | bytes 2359300
  123.8 9.4 %copy-start.11 = (s32[32]{0:T(128)S(1)}, s32[32]{0:T(128)}, u32[]{:S(2)}) copy-start(s32[32]{0:T(128)} %param.26) | copy-start | bytes 388
  123.8 10.0 %copy-start.12 = (s32[32]{0:T(128)S(1)}, s32[32]{0:T(128)}, u32[]{:S(2)}) copy-start(s32[32]{0:T(128)} %param.27) | copy-start | bytes 388
  123.8 101.8 %all-to-all-start.1 = ((bf16[32,512,128]{2,1,0:T(8,128)(2,1)}), bf16[32,512,128]{2,1,0:T(8,128)(2,1)}, u32[]{:S(2)}, u32[]{:S(2)}) async-start(bf16[32,512,128]{2,1,0:T(8,128)(2,1)} %get-tuple-element.14), calls=%async_computation.1 | async-start | bytes 8388608 | tf_op jit(solution)/shard_map/all_to_all | solution.py:196
  131.4 58.5 %all-gather.3.cloned.1.call-start = ((), (), s32[]{:S(2)}) async-start(), calls=%async_computation.5 | async-start | bytes 1179648 | tf_op jit(solution)/shard_map/all_gather | solution.py:198
  132.1 129.7 %all-gather.5.cloned.1.call-start = ((), (), s32[]{:S(2)}) async-start(), calls=%async_computation.6 | async-start | bytes 2359296 | tf_op jit(solution)/shard_map/all_gather | solution.py:207
  253.0 1.5 copy-start.4
  253.0 1.8 copy-start.1
  254.4 14.0 %copy-start.3 = (bf16[64,1024]{1,0:T(8,128)(2,1)S(1)}, bf16[64,1024]{1,0:T(8,128)(2,1)}, u32[]{:S(2)}) copy-start(bf16[64,1024]{1,0:T(8,128)(2,1)} %param.14) | copy-start | bytes 393220
  255.2 15.6 %copy-start.5 = (f32[1024]{0:T(1024)S(1)}, f32[1024]{0:T(1024)}, u32[]{:S(2)}) copy-start(f32[1024]{0:T(1024)} %param.22) | copy-start | bytes 12292
  255.2 15.6 %copy-start.6 = (f32[1024]{0:T(1024)S(1)}, f32[1024]{0:T(1024)}, u32[]{:S(2)}) copy-start(f32[1024]{0:T(1024)} %param.21) | copy-start | bytes 12292
  256.3 12.1 %all-to-all-start.2 = ((bf16[8,64,128]{2,1,0:T(8,128)(2,1)}), bf16[8,64,128]{2,1,0:T(8,128)(2,1)S(1)}, u32[]{:S(2)}, u32[]{:S(2)}) async-start(bf16[8,64,128]{2,1,0:T(8,128)(2,1)} %copy.30), calls=%async_computation.2 | async-start | bytes 262144 | tf_op jit(solution)/shard_map/all_to_all | solution.py:224
  270.5 19.3 %copy-start.10 = (f32[512]{0:T(512)S(1)}, f32[512]{0:T(512)}, u32[]{:S(2)}) copy-start(f32[512]{0:T(512)} %param.18) | copy-start | bytes 6148
  294.5 18.8 %copy-start.7 = (f32[1024]{0:T(1024)S(1)}, f32[1024]{0:T(1024)}, u32[]{:S(2)}) copy-start(f32[1024]{0:T(1024)} %param.20) | copy-start | bytes 12292
  294.5 19.3 %copy-start.8 = (f32[1024]{0:T(1024)S(1)}, f32[1024]{0:T(1024)}, u32[]{:S(2)}) copy-start(f32[1024]{0:T(1024)} %param.24) | copy-start | bytes 12292
  294.5 19.3 %copy-start.9 = (f32[1024]{0:T(1024)S(1)}, f32[1024]{0:T(1024)}, u32[]{:S(2)}) copy-start(f32[1024]{0:T(1024)} %param.23) | copy-start | bytes 12292
Sparse Core Ops, SparseCore 0:
  134.0 55.8 all-gather.2
  191.7 63.9 all-gather.4
